TPU v7x, 512 devices: a whole 4x8x8 slice. The times are simulated.
512 devices in a mesh: context: 32 (over x_hi, y, core), tensor: 16 (over z, x_lo).
Axes of the slice: x: 4 (x_hi: 2, x_lo: 2; x = x_hi * 2 + x_lo), y: 8, z: 8, core: 2. Of those that a mesh axis runs over, the one named last changes fastest.
Arguments:
- projected: bfloat16 [3, 12288, 8192], P(None, 'context', 'tensor'), may hold values from -6 to 6
- taps: float32 [3, 3, 8192], P(None, None, 'tensor'), may hold values from -4 to 4
- filters: bfloat16 [512, 128], P('tensor'), may hold values from -0.5 to 0.5
- skip: float32 [8192], P('tensor'), may hold values from -4 to 4
- out_weight: bfloat16 [8192, 8192], P('tensor', 'context'), may hold values from -0.125 to 0.125
- positions: int32 [128], replicated, may hold values from 0 to 12287
Outputs:
- mixed: bfloat16 [12288, 8192], P('context', 'tensor')
- variant_states: bfloat16 [128, 8192], P('context', 'tensor')
All inputs are finite; a program needn't handle non-finite values.
Results may differ from a plain program's by a relative error of at most 0.018.
Values may be sent and summed in bfloat16 or wider, within the bound.
No kernel may reach another device: no remote copies, remote signals or barrier semaphores. Data moves between devices by JAX's collectives and lax.ppermute only.
A program may use at most 128 MiB of HBM per device.

v0:
```python
import jax
import jax.numpy as jnp
from jax import lax
from jax.sharding import PartitionSpec as P

FLT = 128
GROUP = 16
SHORT = 3


def shifted(array, axis, by):
    size = lax.axis_size(axis)
    pairs = [(i, i + by) for i in range(size) if 0 <= i + by < size]
    return lax.ppermute(array, axis, pairs)


def short_filter(extended, weights, count):
    lags = SHORT - 1
    total = jnp.zeros((extended.shape[0], count, extended.shape[2]), jnp.float32)
    for lag in range(SHORT):
        total = total + weights[:, lag, None, :] * extended[
            :, lags - lag : lags - lag + count, :
        ].astype(jnp.float32)
    return total


def banded_filters(filters, rows):
    local_groups = filters.shape[0]
    span = FLT - 1 + rows
    reversed_taps = jnp.flip(filters, axis=1)
    padded_taps = jnp.concatenate(
        [reversed_taps, jnp.zeros((local_groups, rows), filters.dtype)], axis=1
    )
    tiled = jnp.tile(padded_taps, (1, rows))
    return tiled[:, : rows * span].reshape(local_groups, rows, span)


def on_device(projected, taps, filters, skip, out_weight, positions):
    rows = projected.shape[1]
    width = projected.shape[2]
    lags = SHORT - 1
    reach = FLT - 1
    rim = shifted(projected[:, rows - lags :, :], "context", 1)
    feat = short_filter(jnp.concatenate([rim, projected], axis=1), taps, rows)
    query = feat[0]
    product = (feat[1] * feat[2]).astype(jnp.bfloat16)
    prior = shifted(product[rows - reach :], "context", 1)
    extended = jnp.concatenate([prior, product], axis=0)
    span = reach + rows
    toeplitz = banded_filters(filters, rows)
    local_groups = filters.shape[0]
    conv = jnp.einsum(
        "gim,mgc->igc",
        toeplitz,
        extended.reshape(span, local_groups, GROUP),
        preferred_element_type=jnp.float32,
    ).reshape(rows, width)
    conv = conv + skip[None, :] * product.astype(jnp.float32)
    gated = (query * conv).astype(jnp.bfloat16)
    terms = jnp.dot(
        gated,
        lax.all_gather(out_weight, "context", axis=1, tiled=True),
        preferred_element_type=jnp.float32,
    )
    mixed = lax.psum_scatter(terms.astype(jnp.bfloat16), "tensor", scatter_dimension=1, tiled=True)
    offset = lax.axis_index("context") * rows
    local_sites = positions - offset
    one_hot = (local_sites[:, None] == jnp.arange(rows, dtype=jnp.int32)[None, :]).astype(
        jnp.bfloat16
    )
    picked_terms = jnp.dot(one_hot, mixed, preferred_element_type=jnp.float32)
    variant_states = lax.psum_scatter(
        picked_terms.astype(jnp.bfloat16), "context", scatter_dimension=0, tiled=True
    )
    return (mixed, variant_states)


def solution(mesh):
    return jax.shard_map(
        on_device,
        mesh=mesh,
        in_specs=(
            P(None, "context", "tensor"),
            P(None, None, "tensor"),
            P("tensor", None),
            P("tensor"),
            P("tensor", "context"),
            P(),
        ),
        out_specs=(P("context", "tensor"), P("context", "tensor")),
        check_vma=False,
    )
```

profile of v0, /device:TPU:1, one launch (start us, length us, event | category | flops | bytes accessed | tf_op | source)
XLA Modules:
  0.0 539.2 jit_solution(17481667144014978394)
XLA Ops:
  7.2 0.7 all-gather.2.cloned.1.call-update
  7.9 0.8 slice.38
  8.7 4.6 collective-permute-start
  13.3 0.9 fusion.8
  14.2 0.6 copy.21
  14.8 0.8 rev.4
  15.6 5.4 %tile.4 = bf16[32,384,512]{2,1,0:T(8,128)(2,1)} broadcast(bf16[32,512]{1,0:T(8,128)(2,1)S(1)} %concatenate.11), dimensions={0,2} | broadcast | bytes 12615680 | tf_op jit(solution)/shard_map/tile | solution.py:34
  21.0 12.0 %copy.17 = bf16[4,8,384,512]{3,1,2,0:T(8,128)(2,1)S(1)} copy(bf16[4,8,384,512]{3,2,1,0:T(8,128)(2,1)} %bitcast.33) | data formatting | bytes 25165824
  33.0 5.2 slice.54
  38.2 29.3 %reshape.23 = bf16[32,384,511]{2,1,0:T(8,128)(2,1)} reshape(bf16[32,196224]{1,0:T(8,128)(2,1)} %slice.54) | data formatting | bytes 25116672 | tf_op jit(solution)/shard_map/reshape | solution.py:35
  67.5 0.6 copy-done.1
  68.1 1.5 multiply_add_fusion
  69.8 2.1 collective-permute-start.1
  72.0 3.5 collective-permute-done.1
  75.6 1.0 copy.12
  76.6 8.3 %fusion.9 = f32[32,16,384]{2,1,0:T(8,128)S(1)} fusion(bf16[511,32,16]{0,2,1:T(8,128)(2,1)} %bitcast.36, bf16[32,384,511]{2,1,0:T(8,128)(2,1)} %reshape.23), kind=kOutput, calls=%fused_computation.24 | convolution fusion | flops 200933376 | bytes 13868032 | tf_op jit(solution)/shard_map/gim,mgc->igc/dot_general | solution.py:52
  84.9 1.2 copy.13
  86.1 44.6 %all-gather.2.cloned.1.call-done = bf16[512,8192]{1,0:T(8,128)(2,1)} async-done(((bf16[512,256]{1,0:T(8,128)(2,1)}), bf16[512,8192]{1,0:T(8,128)(2,1)}) %all-gather.2.cloned.1.call-update) | async-done | bytes 8388624 | tf_op jit(solution)/shard_map/all_gather | solution.py:62
  130.7 9.8 %convolution_convert_fusion = bf16[384,8192]{1,0:T(8,128)(2,1)} fusion(bf16[512,8192]{1,0:T(8,128)(2,1)} %all-gather.2.cloned.1.call-done, f32[3,384,512]{2,1,0:T(8,128)S(1)} %multiply_add_fusion, f32[384,512]{1,0:T(8,128)} %copy.13, f32[512]{0:T(512)S(1)} %copy-done.2, bf16[1,384,512]{2,1,0:T(8,128)(2,1)S(1)} %fusion.1), kind=kOutput, calls=%fused_computation | convolution fusion | flops 3225354240 | bytes 16648192 | tf_op jit(solution)/shard_map/dot_general | solution.py:60
  141.1 138.5 %reduce-scatter.2.cloned.1.call-done = bf16[384,512]{1,0:T(8,128)(2,1)} async-done(((bf16[384,8192]{1,0:T(8,128)(2,1)}), bf16[384,512]{1,0:T(8,128)(2,1)}) %reduce-scatter.2.cloned.1.call-update) | async-done | bytes 393232 | tf_op jit(solution)/shard_map/reduce_scatter | solution.py:65
  279.6 1.9 convolution_convert_fusion.1
  281.5 1.3 dynamic-slice
  283.4 248.0 %all-reduce.4.cloned.1.call-done = bf16[128,512]{1,0:T(8,128)(2,1)} async-done(((bf16[128,512]{1,0:T(8,128)(2,1)}), bf16[128,512]{1,0:T(8,128)(2,1)}) %all-reduce.4.cloned.1.call-update) | async-done | bytes 131088
  531.4 1.3 constant_dynamic-slice_fusion
  (20 shorter events, 1.1 us)
Async XLA Ops:
  7.2 123.5 %all-gather.2.cloned.1.call-start = ((), (), s32[]{:S(2)}) async-start(), calls=%async_computation.1 | async-start | bytes 8650752 | tf_op jit(solution)/shard_map/all_gather | solution.py:62
  7.9 271.7 %reduce-scatter.2.cloned.1.call-start = ((), (), s32[]{:S(2)}) async-start(), calls=%async_computation.2 | async-start | bytes 6684672 | tf_op jit(solution)/shard_map/reduce_scatter | solution.py:65
  8.7 58.8 %collective-permute-start = (bf16[3,2,512]{2,1,0:T(2,128)(2,1)S(1)}, bf16[3,2,512]{2,1,0:T(2,128)(2,1)S(1)}, u32[]{:S(2)}, u32[]{:S(2)}) collective-permute-start(bf16[3,2,512]{2,1,0:T(2,128)(2,1)S(1)} %slice.38), channel_id=1, source_target_pairs={{0,16},{16,32},{32,48},{48,64},{64,80},{80,96},{96,112},{112,128},... | collective-permute-start | bytes 18440 | tf_op jit(solution)/shard_map/ppermute | solution.py:14
  38.2 29.9 %copy-start = (bf16[3,384,512]{2,1,0:T(8,128)(2,1)S(1)}, bf16[3,384,512]{2,1,0:T(8,128)(2,1)}, u32[]{:S(2)}) copy-start(bf16[3,384,512]{2,1,0:T(8,128)(2,1)} %param.6) | copy-start | bytes 3538948
  67.5 0.6 copy-start.1
  69.8 5.7 %collective-permute-start.1 = (bf16[127,512]{1,0:T(8,128)(2,1)S(1)}, bf16[127,512]{1,0:T(8,128)(2,1)S(1)}, u32[]{:S(2)}, u32[]{:S(2)}) collective-permute-start(bf16[127,512]{1,0:T(8,128)(2,1)S(1)} %slice_bitcast_fusion.1), channel_id=1, source_target_pairs={{0,16},{16,32},{32,48},{48,64},{64,80},{80,96},{96,112},{112,128},... | collective-permute-start | bytes 390152 | tf_op jit(solution)/shard_map/ppermute | solution.py:14
  76.6 54.1 %copy-start.2 = (f32[512]{0:T(512)S(1)}, f32[512]{0:T(512)}, u32[]{:S(2)}) copy-start(f32[512]{0:T(512)} %param.9) | copy-start | bytes 6148
  140.5 0.7 copy-start.3
  140.5 390.9 %all-reduce.4.cloned.1.call-start = ((), (), s32[]{:S(2)}) async-start(), calls=%async_computation.3 | async-start | bytes 262144
Sparse Core Ops, SparseCore 0:
  11.1 119.4 all-gather.1
  140.6 138.9 reduce-scatter.1
  282.5 248.8 all-reduce.3
where the time goes:
time: 540 us; the launch traced here: 539 us
  waiting for transfers between devices  435 us (81%)
  local copies, waits for them, and re-layouts  60.9 us (11%)
  matrix products  20 us (4%)
  between operations  14.5 us (3%)
  starting transfers between devices  6.81 us (1%)
    unnamed x4, waiting for transfers between devices  249 us
    reduce_scatter x1, waiting for transfers between devices, on_device(): lax.psum_scatter(terms.astype(jnp.bfloat16), 'tensor', scatter_dimension=...  138 us
    all_gather x1, waiting for transfers between devices, on_device(): lax.all_gather(out_weight, 'context', axis=1, tiled=True)  44.6 us
    reshape x1, local copies, waits for them, and re-layouts, banded_filters(): return tiled[:, :rows * span].reshape(local_groups, rows, span)  29.3 us
    unnamed x13, local copies, waits for them, and re-layouts  16.4 us
  transfers between devices with their start and end apart: 5, of which 4 were waited for; matrix products, arithmetic and copies ran while one was open for 13% of the time, Pallas kernels for 0%

commit v1 on v0

--- a/solution.py
+++ b/solution.py
@@ -12,6 +12,23 @@
     size = lax.axis_size(axis)
     pairs = [(i, i + by) for i in range(size) if 0 <= i + by < size]
     return lax.ppermute(array, axis, pairs)
+
+
+def halving_scatter(rows, axis):
+    size = lax.axis_size(axis)
+    if size & (size - 1) or rows.shape[0] % size:
+        return lax.psum_scatter(rows, axis, scatter_dimension=0, tiled=True)
+    me = lax.axis_index(axis)
+    step = size // 2
+    while step >= 1:
+        half = rows.shape[0] // 2
+        bit = (me // step) % 2
+        keep = lax.dynamic_slice_in_dim(rows, bit * half, half, 0)
+        send = lax.dynamic_slice_in_dim(rows, (1 - bit) * half, half, 0)
+        pairs = [(i, i ^ step) for i in range(size)]
+        rows = keep + lax.ppermute(send, axis, pairs)
+        step //= 2
+    return rows
 
 
 def short_filter(extended, weights, count):
@@ -69,9 +86,7 @@
         jnp.bfloat16
     )
     picked_terms = jnp.dot(one_hot, mixed, preferred_element_type=jnp.float32)
-    variant_states = lax.psum_scatter(
-        picked_terms.astype(jnp.bfloat16), "context", scatter_dimension=0, tiled=True
-    )
+    variant_states = halving_scatter(picked_terms.astype(jnp.bfloat16), "context")
     return (mixed, variant_states)
 
 

time: 540 us -> 322 us (0.60)
  waiting for transfers between devices: 435 us -> 193 us
  starting transfers between devices: 6.81 us -> 33.7 us
    unnamed x4 -> x2, waiting for transfers between devices: 249 us -> 0.7 us
    ppermute x0 -> x5, starting transfers between devices: none -> 26.9 us  [halving_scatter(): rows = keep + lax.ppermute(send, axis, pairs)]
    ppermute x0 -> x5, waiting for transfers between devices: none -> 6.25 us  [halving_scatter(): rows = keep + lax.ppermute(send, axis, pairs)]
    unnamed x13 -> x11, local copies, waits for them, and re-layouts: 16.4 us -> 13.8 us
  transfers between devices with their start and end apart: 5 -> 9, of which waited for: 4 -> 8; matrix products, arithmetic and copies ran while one was open for 13% -> 21% of each run, Pallas kernels for 0% -> 0%
where the time goes in v1:
time: 322 us
  waiting for transfers between devices  193 us (60%)
  local copies, waits for them, and re-layouts  58.4 us (18%)
  starting transfers between devices  33.7 us (10%)
  matrix products  19.4 us (6%)
  between operations  14.4 us (4%)
    reduce_scatter x1, waiting for transfers between devices, on_device(): lax.psum_scatter(terms.astype(jnp.bfloat16), 'tensor', scatter_dimension=...  138 us
    all_gather x1, waiting for transfers between devices, on_device(): lax.all_gather(out_weight, 'context', axis=1, tiled=True)  44.6 us
    reshape x1, local copies, waits for them, and re-layouts, banded_filters(): return tiled[:, :rows * span].reshape(local_groups, rows, span)  29.3 us
    ppermute x5, starting transfers between devices, halving_scatter(): rows = keep + lax.ppermute(send, axis, pairs)  26.9 us
    unnamed x11, local copies, waits for them, and re-layouts  13.8 us
    dot_general x1, matrix products, on_device(): jnp.dot(gated, lax.all_gather(out_weight, 'context', axis=1, tiled=True),...  9.78 us
    dot_general x1, matrix products, on_device(): jnp.einsum('gim,mgc->igc', toeplitz, extended.reshape(span, local_groups,...  8.33 us
    ppermute x2, starting transfers between devices, shifted(): return lax.ppermute(array, axis, pairs)  6.72 us
  transfers between devices with their start and end apart: 9, of which 8 were waited for; matrix products, arithmetic and copies ran while one was open for 21% of the time, Pallas kernels for 0%

profile of v1, /device:TPU:1, one launch (start us, length us, event | category | flops | bytes accessed | tf_op | source)
XLA Modules:
  0.0 321.8 jit_solution(6811182927905983735)
XLA Ops:
  8.7 4.6 %collective-permute-start = (bf16[3,2,512]{2,1,0:T(2,128)(2,1)S(1)}, bf16[3,2,512]{2,1,0:T(2,128)(2,1)S(1)}, u32[]{:S(2)}, u32[]{:S(2)}) collective-permute-start(bf16[3,2,512]{2,1,0:T(2,128)(2,1)S(1)} %slice.38), channel_id=1, source_target_pairs={{0,16},{16,32},{32,48},{48,64},{64,80},{80,96},{96,112},{112,128},... | collective-permute-start | bytes 18440 | tf_op jit(solution)/shard_map/ppermute | solution.py:14
  15.6 5.4 %tile.4 = bf16[32,384,512]{2,1,0:T(8,128)(2,1)} broadcast(bf16[32,512]{1,0:T(8,128)(2,1)S(1)} %concatenate.11), dimensions={0,2} | broadcast | bytes 12615680 | tf_op jit(solution)/shard_map/tile | solution.py:51
  21.0 12.0 %copy.15 = bf16[4,8,384,512]{3,1,2,0:T(8,128)(2,1)S(1)} copy(bf16[4,8,384,512]{3,2,1,0:T(8,128)(2,1)} %bitcast.32) | data formatting | bytes 25165824
  33.0 5.1 %slice.54 = bf16[32,196224]{1,0:T(8,128)(2,1)} slice(bf16[32,196608]{1,0:T(8,128)(2,1)S(1)} %bitcast.33), slice={[0:32], [0:196224]} | slice | bytes 25116672 | tf_op jit(solution)/shard_map/slice | solution.py:52
  38.2 29.3 %reshape.23 = bf16[32,384,511]{2,1,0:T(8,128)(2,1)} reshape(bf16[32,196224]{1,0:T(8,128)(2,1)} %slice.54) | data formatting | bytes 25116672 | tf_op jit(solution)/shard_map/reshape | solution.py:52
  68.1 1.5 multiply_add_fusion
  69.8 2.1 collective-permute-start.1
  72.0 3.4 %collective-permute-done.1 = bf16[127,512]{1,0:T(8,128)(2,1)S(1)} collective-permute-done((bf16[127,512]{1,0:T(8,128)(2,1)S(1)}, bf16[127,512]{1,0:T(8,128)(2,1)S(1)}, u32[]{:S(2)}, u32[]{:S(2)}) %collective-permute-start.1) | collective-permute-done | bytes 130080 | tf_op jit(solution)/shard_map/ppermute | solution.py:14
  75.5 1.0 copy.10
  76.6 8.3 %fusion.9 = f32[32,16,384]{2,1,0:T(8,128)S(1)} fusion(bf16[511,32,16]{0,2,1:T(8,128)(2,1)} %bitcast.35, bf16[32,384,511]{2,1,0:T(8,128)(2,1)} %reshape.23), kind=kOutput, calls=%fused_computation.33 | convolution fusion | flops 200933376 | bytes 13868032 | tf_op jit(solution)/shard_map/gim,mgc->igc/dot_general | solution.py:69
  84.9 1.2 copy.11
  86.1 44.6 %all-gather.2.cloned.1.call-done = bf16[512,8192]{1,0:T(8,128)(2,1)} async-done(((bf16[512,256]{1,0:T(8,128)(2,1)}), bf16[512,8192]{1,0:T(8,128)(2,1)}) %all-gather.2.cloned.1.call-update) | async-done | bytes 8388624 | tf_op jit(solution)/shard_map/all_gather | solution.py:79
  130.7 9.8 %convolution_convert_fusion = bf16[384,8192]{1,0:T(8,128)(2,1)} fusion(bf16[512,8192]{1,0:T(8,128)(2,1)} %all-gather.2.cloned.1.call-done, f32[3,384,512]{2,1,0:T(8,128)S(1)} %multiply_add_fusion, f32[384,512]{1,0:T(8,128)} %copy.11, f32[512]{0:T(512)S(1)} %copy-done.2, bf16[1,384,512]{2,1,0:T(8,128)(2,1)S(1)} %fusion.1), kind=kOutput, calls=%fused_computation | convolution fusion | flops 3225354240 | bytes 16648192 | tf_op jit(solution)/shard_map/dot_general | solution.py:77
  141.1 138.4 %reduce-scatter.2.cloned.1.call-done = bf16[384,512]{1,0:T(8,128)(2,1)} async-done(((bf16[384,8192]{1,0:T(8,128)(2,1)}), bf16[384,512]{1,0:T(8,128)(2,1)}) %reduce-scatter.2.cloned.1.call-update) | async-done | bytes 393232 | tf_op jit(solution)/shard_map/reduce_scatter | solution.py:82
  279.6 1.3 convolution_convert_fusion.1
  280.8 4.7 %collective-permute-start.2 = (bf16[64,512]{1,0:T(8,128)(2,1)S(1)}, bf16[64,512]{1,0:T(8,128)(2,1)S(1)}, u32[]{:S(2)}, u32[]{:S(2)}) collective-permute-start(bf16[64,512]{1,0:T(8,128)(2,1)S(1)} %constant_dynamic-slice_fusion.4), channel_id=1, source_target_pairs={{0,256},{16,272},{32,288},{48,304},{64,320},{80,336},{96,352},{112... | collective-permute-start | bytes 196616 | tf_op jit(solution)/shard_map/ppermute | solution.py:29
  285.6 1.7 collective-permute-done.2
  287.4 7.2 %collective-permute-start.3 = (bf16[32,512]{1,0:T(8,128)(2,1)S(1)}, bf16[32,512]{1,0:T(8,128)(2,1)S(1)}, u32[]{:S(2)}, u32[]{:S(2)}) collective-permute-start(bf16[32,512]{1,0:T(8,128)(2,1)S(1)} %constant_dynamic-slice_fusion.3), channel_id=1, source_target_pairs={{0,128},{16,144},{32,160},{48,176},{64,192},{80,208},{96,224},{112... | collective-permute-start | bytes 98312 | tf_op jit(solution)/shard_map/ppermute | solution.py:29
  294.7 1.3 collective-permute-done.3
  296.0 4.4 %collective-permute-start.4 = (bf16[16,512]{1,0:T(8,128)(2,1)S(1)}, bf16[16,512]{1,0:T(8,128)(2,1)S(1)}, u32[]{:S(2)}, u32[]{:S(2)}) collective-permute-start(bf16[16,512]{1,0:T(8,128)(2,1)S(1)} %constant_dynamic-slice_fusion.2), channel_id=1, source_target_pairs={{0,64},{16,80},{32,96},{48,112},{64,0},{80,16},{96,32},{112,48},{1... | collective-permute-start | bytes 49160 | tf_op jit(solution)/shard_map/ppermute | solution.py:29
  300.5 1.1 collective-permute-done.4
  301.6 3.0 collective-permute-start.5
  304.7 1.3 collective-permute-done.5
  306.0 7.5 %collective-permute-start.6 = (bf16[4,512]{1,0:T(4,128)(2,1)S(1)}, bf16[4,512]{1,0:T(4,128)(2,1)S(1)}, u32[]{:S(2)}, u32[]{:S(2)}) collective-permute-start(bf16[4,512]{1,0:T(4,128)(2,1)S(1)} %constant_dynamic-slice_fusion), channel_id=1, source_target_pairs={{0,16},{16,0},{32,48},{48,32},{64,80},{80,64},{96,112},{112,96},{1... | collective-permute-start | bytes 12296 | tf_op jit(solution)/shard_map/ppermute | solution.py:29
  (35 shorter events, 6.8 us)
Async XLA Ops:
  7.2 123.5 %all-gather.2.cloned.1.call-start = ((), (), s32[]{:S(2)}) async-start(), calls=%async_computation.1 | async-start | bytes 8650752 | tf_op jit(solution)/shard_map/all_gather | solution.py:79
  7.9 271.7 %reduce-scatter.2.cloned.1.call-start = ((), (), s32[]{:S(2)}) async-start(), calls=%async_computation.2 | async-start | bytes 6684672 | tf_op jit(solution)/shard_map/reduce_scatter | solution.py:82
  8.7 58.8 %collective-permute-start = (bf16[3,2,512]{2,1,0:T(2,128)(2,1)S(1)}, bf16[3,2,512]{2,1,0:T(2,128)(2,1)S(1)}, u32[]{:S(2)}, u32[]{:S(2)}) collective-permute-start(bf16[3,2,512]{2,1,0:T(2,128)(2,1)S(1)} %slice.38), channel_id=1, source_target_pairs={{0,16},{16,32},{32,48},{48,64},{64,80},{80,96},{96,112},{112,128},... | collective-permute-start | bytes 18440 | tf_op jit(solution)/shard_map/ppermute | solution.py:14
  38.2 29.9 %copy-start = (bf16[3,384,512]{2,1,0:T(8,128)(2,1)S(1)}, bf16[3,384,512]{2,1,0:T(8,128)(2,1)}, u32[]{:S(2)}) copy-start(bf16[3,384,512]{2,1,0:T(8,128)(2,1)} %param.6) | copy-start | bytes 3538948
  67.5 0.6 copy-start.1
  69.8 5.7 %collective-permute-start.1 = (bf16[127,512]{1,0:T(8,128)(2,1)S(1)}, bf16[127,512]{1,0:T(8,128)(2,1)S(1)}, u32[]{:S(2)}, u32[]{:S(2)}) collective-permute-start(bf16[127,512]{1,0:T(8,128)(2,1)S(1)} %slice_bitcast_fusion.1), channel_id=1, source_target_pairs={{0,16},{16,32},{32,48},{48,64},{64,80},{80,96},{96,112},{112,128},... | collective-permute-start | bytes 390152 | tf_op jit(solution)/shard_map/ppermute | solution.py:14
  76.6 54.1 %copy-start.2 = (f32[512]{0:T(512)S(1)}, f32[512]{0:T(512)}, u32[]{:S(2)}) copy-start(f32[512]{0:T(512)} %param.9) | copy-start | bytes 6148
  140.5 0.7 copy-start.3
  280.8 6.5 %collective-permute-start.2 = (bf16[64,512]{1,0:T(8,128)(2,1)S(1)}, bf16[64,512]{1,0:T(8,128)(2,1)S(1)}, u32[]{:S(2)}, u32[]{:S(2)}) collective-permute-start(bf16[64,512]{1,0:T(8,128)(2,1)S(1)} %constant_dynamic-slice_fusion.4), channel_id=1, source_target_pairs={{0,256},{16,272},{32,288},{48,304},{64,320},{80,336},{96,352},{112... | collective-permute-start | bytes 196616 | tf_op jit(solution)/shard_map/ppermute | solution.py:29
  287.4 8.6 %collective-permute-start.3 = (bf16[32,512]{1,0:T(8,128)(2,1)S(1)}, bf16[32,512]{1,0:T(8,128)(2,1)S(1)}, u32[]{:S(2)}, u32[]{:S(2)}) collective-permute-start(bf16[32,512]{1,0:T(8,128)(2,1)S(1)} %constant_dynamic-slice_fusion.3), channel_id=1, source_target_pairs={{0,128},{16,144},{32,160},{48,176},{64,192},{80,208},{96,224},{112... | collective-permute-start | bytes 98312 | tf_op jit(solution)/shard_map/ppermute | solution.py:29
  296.0 5.5 %collective-permute-start.4 = (bf16[16,512]{1,0:T(8,128)(2,1)S(1)}, bf16[16,512]{1,0:T(8,128)(2,1)S(1)}, u32[]{:S(2)}, u32[]{:S(2)}) collective-permute-start(bf16[16,512]{1,0:T(8,128)(2,1)S(1)} %constant_dynamic-slice_fusion.2), channel_id=1, source_target_pairs={{0,64},{16,80},{32,96},{48,112},{64,0},{80,16},{96,32},{112,48},{1... | collective-permute-start | bytes 49160 | tf_op jit(solution)/shard_map/ppermute | solution.py:29
  301.6 4.4 %collective-permute-start.5 = (bf16[8,512]{1,0:T(8,128)(2,1)S(1)}, bf16[8,512]{1,0:T(8,128)(2,1)S(1)}, u32[]{:S(2)}, u32[]{:S(2)}) collective-permute-start(bf16[8,512]{1,0:T(8,128)(2,1)S(1)} %constant_dynamic-slice_fusion.1), channel_id=1, source_target_pairs={{0,32},{16,48},{32,0},{48,16},{64,96},{80,112},{96,64},{112,80},{1... | collective-permute-start | bytes 24584 | tf_op jit(solution)/shard_map/ppermute | solution.py:29
  306.0 8.3 %collective-permute-start.6 = (bf16[4,512]{1,0:T(4,128)(2,1)S(1)}, bf16[4,512]{1,0:T(4,128)(2,1)S(1)}, u32[]{:S(2)}, u32[]{:S(2)}) collective-permute-start(bf16[4,512]{1,0:T(4,128)(2,1)S(1)} %constant_dynamic-slice_fusion), channel_id=1, source_target_pairs={{0,16},{16,0},{32,48},{48,32},{64,80},{80,64},{96,112},{112,96},{1... | collective-permute-start | bytes 12296 | tf_op jit(solution)/shard_map/ppermute | solution.py:29
Sparse Core Ops, SparseCore 0:
  11.1 119.4 all-gather.1
  140.6 138.9 reduce-scatter.1

commit v2 on v1

--- a/solution.py
+++ b/solution.py
@@ -1,7 +1,8 @@
 import jax
 import jax.numpy as jnp
 from jax import lax
-from jax.sharding import PartitionSpec as P
+import numpy as np
+from jax.sharding import Mesh, PartitionSpec as P
 
 FLT = 128
 GROUP = 16
@@ -79,7 +80,8 @@
         lax.all_gather(out_weight, "context", axis=1, tiled=True),
         preferred_element_type=jnp.float32,
     )
-    mixed = lax.psum_scatter(terms.astype(jnp.bfloat16), "tensor", scatter_dimension=1, tiled=True)
+    mixed = lax.psum_scatter(terms.astype(jnp.bfloat16), "z", scatter_dimension=1, tiled=True)
+    mixed = lax.psum_scatter(mixed, "x_lo", scatter_dimension=1, tiled=True)
     offset = lax.axis_index("context") * rows
     local_sites = positions - offset
     one_hot = (local_sites[:, None] == jnp.arange(rows, dtype=jnp.int32)[None, :]).astype(
@@ -90,18 +92,25 @@
     return (mixed, variant_states)
 
 
+def split_mesh(mesh):
+    devices = np.asarray(mesh.devices)
+    context, tensor = devices.shape
+    return Mesh(devices.reshape(context, tensor // 2, 2), ("context", "z", "x_lo"))
+
+
 def solution(mesh):
+    tensor = ("z", "x_lo")
     return jax.shard_map(
         on_device,
-        mesh=mesh,
+        mesh=split_mesh(mesh),
         in_specs=(
-            P(None, "context", "tensor"),
-            P(None, None, "tensor"),
-            P("tensor", None),
-            P("tensor"),
-            P("tensor", "context"),
+            P(None, "context", tensor),
+            P(None, None, tensor),
+            P(tensor, None),
+            P(tensor),
+            P(tensor, "context"),
             P(),
         ),
-        out_specs=(P("context", "tensor"), P("context", "tensor")),
+        out_specs=(P("context", tensor), P("context", tensor)),
         check_vma=False,
     )

time: 322 us -> 284 us (0.88)
  waiting for transfers between devices: 193 us -> 157 us
    reduce_scatter x1 -> x2, waiting for transfers between devices: 138 us -> 102 us  [the longest x1 74.9 us: on_device(): lax.psum_scatter(terms.astype(jnp.bfloat16), 'z', scatter_dimension=1, ti...]
  transfers between devices with their start and end apart: 9 -> 10, of which waited for: 8 -> 9; matrix products, arithmetic and copies ran while one was open for 21% -> 24% of each run, Pallas kernels for 0% -> 0%
where the time goes in v2:
time: 284 us
  waiting for transfers between devices  157 us (55%)
  local copies, waits for them, and re-layouts  57.8 us (20%)
  starting transfers between devices  32.6 us (11%)
  matrix products  19.4 us (7%)
  between operations  14.1 us (5%)
    reduce_scatter x1, waiting for transfers between devices, on_device(): lax.psum_scatter(terms.astype(jnp.bfloat16), 'z', scatter_dimension=1, ti...  74.9 us
    all_gather x1, waiting for transfers between devices, on_device(): lax.all_gather(out_weight, 'context', axis=1, tiled=True)  44.6 us
    reshape x1, local copies, waits for them, and re-layouts, banded_filters(): return tiled[:, :rows * span].reshape(local_groups, rows, span)  29.3 us
    reduce_scatter x1, waiting for transfers between devices, on_device(): mixed = lax.psum_scatter(mixed, 'x_lo', scatter_dimension=1, tiled=True)  26.7 us
    ppermute x5, starting transfers between devices, halving_scatter(): rows = keep + lax.ppermute(send, axis, pairs)  25.8 us
    unnamed x11, local copies, waits for them, and re-layouts  13.2 us
    dot_general x1, matrix products, on_device(): jnp.dot(gated, lax.all_gather(out_weight, 'context', axis=1, tiled=True),...  9.78 us
    dot_general x1, matrix products, on_device(): jnp.einsum('gim,mgc->igc', toeplitz, extended.reshape(span, local_groups,...  8.33 us
  transfers between devices with their start and end apart: 10, of which 9 were waited for; matrix products, arithmetic and copies ran while one was open for 24% of the time, Pallas kernels for 0%

profile of v2, /device:TPU:1, one launch (start us, length us, event | category | flops | bytes accessed | tf_op | source)
XLA Modules:
  0.0 283.6 jit_solution(7934019625295655519)
XLA Ops:
  8.7 4.6 %collective-permute-start = (bf16[3,2,512]{2,1,0:T(2,128)(2,1)S(1)}, bf16[3,2,512]{2,1,0:T(2,128)(2,1)S(1)}, u32[]{:S(2)}, u32[]{:S(2)}) collective-permute-start(bf16[3,2,512]{2,1,0:T(2,128)(2,1)S(1)} %slice.38), channel_id=1, source_target_pairs={{0,16},{16,32},{32,48},{48,64},{64,80},{80,96},{96,112},{112,128},... | collective-permute-start | bytes 18440 | tf_op jit(solution)/shard_map/ppermute | solution.py:15
  15.6 5.4 %tile.4 = bf16[32,384,512]{2,1,0:T(8,128)(2,1)} broadcast(bf16[32,512]{1,0:T(8,128)(2,1)S(1)} %concatenate.11), dimensions={0,2} | broadcast | bytes 12615680 | tf_op jit(solution)/shard_map/tile | solution.py:52
  21.0 12.0 %copy.15 = bf16[4,8,384,512]{3,1,2,0:T(8,128)(2,1)S(1)} copy(bf16[4,8,384,512]{3,2,1,0:T(8,128)(2,1)} %bitcast.32) | data formatting | bytes 25165824
  33.0 5.1 %slice.54 = bf16[32,196224]{1,0:T(8,128)(2,1)} slice(bf16[32,196608]{1,0:T(8,128)(2,1)S(1)} %bitcast.33), slice={[0:32], [0:196224]} | slice | bytes 25116672 | tf_op jit(solution)/shard_map/slice | solution.py:53
  38.2 29.3 %reshape.23 = bf16[32,384,511]{2,1,0:T(8,128)(2,1)} reshape(bf16[32,196224]{1,0:T(8,128)(2,1)} %slice.54) | data formatting | bytes 25116672 | tf_op jit(solution)/shard_map/reshape | solution.py:53
  68.1 1.5 multiply_add_fusion
  69.8 2.1 collective-permute-start.1
  72.0 3.4 %collective-permute-done.1 = bf16[127,512]{1,0:T(8,128)(2,1)S(1)} collective-permute-done((bf16[127,512]{1,0:T(8,128)(2,1)S(1)}, bf16[127,512]{1,0:T(8,128)(2,1)S(1)}, u32[]{:S(2)}, u32[]{:S(2)}) %collective-permute-start.1) | collective-permute-done | bytes 130080 | tf_op jit(solution)/shard_map/ppermute | solution.py:15
  76.6 8.3 %fusion.9 = f32[32,16,384]{2,1,0:T(8,128)S(1)} fusion(bf16[511,32,16]{0,2,1:T(8,128)(2,1)} %bitcast.35, bf16[32,384,511]{2,1,0:T(8,128)(2,1)} %reshape.23), kind=kOutput, calls=%fused_computation.33 | convolution fusion | flops 200933376 | bytes 13868032 | tf_op jit(solution)/shard_map/gim,mgc->igc/dot_general | solution.py:70
  84.9 1.2 copy.11
  86.1 44.6 %all-gather.2.cloned.1.call-done = bf16[512,8192]{1,0:T(8,128)(2,1)} async-done(((bf16[512,256]{1,0:T(8,128)(2,1)}), bf16[512,8192]{1,0:T(8,128)(2,1)}) %all-gather.2.cloned.1.call-update) | async-done | bytes 8388624 | tf_op jit(solution)/shard_map/all_gather | solution.py:80
  130.7 9.8 %convolution_convert_fusion = bf16[384,8192]{1,0:T(8,128)(2,1)} fusion(bf16[512,8192]{1,0:T(8,128)(2,1)} %all-gather.2.cloned.1.call-done, f32[3,384,512]{2,1,0:T(8,128)S(1)} %multiply_add_fusion, f32[384,512]{1,0:T(8,128)} %copy.11, f32[512]{0:T(512)S(1)} %copy-done.2, bf16[1,384,512]{2,1,0:T(8,128)(2,1)S(1)} %fusion.1), kind=kOutput, calls=%fused_computation | convolution fusion | flops 3225354240 | bytes 16648192 | tf_op jit(solution)/shard_map/dot_general | solution.py:78
  140.5 74.9 %reduce-scatter.3.cloned.1.call-done = bf16[384,1024]{1,0:T(8,128)(2,1)} async-done(((bf16[384,8192]{1,0:T(8,128)(2,1)}), bf16[384,1024]{1,0:T(8,128)(2,1)}) %reduce-scatter.3.cloned.1.call-update) | async-done | bytes 786448 | tf_op jit(solution)/shard_map/reduce_scatter | solution.py:83
  215.5 26.7 %reduce-scatter.5.cloned.1.call-done = bf16[384,512]{1,0:T(8,128)(2,1)} async-done(((bf16[384,1024]{1,0:T(8,128)(2,1)}), bf16[384,512]{1,0:T(8,128)(2,1)}) %reduce-scatter.5.cloned.1.call-update) | async-done | bytes 393232 | tf_op jit(solution)/shard_map/reduce_scatter | solution.py:84
  242.2 1.3 convolution_convert_fusion.1
  243.5 4.3 %collective-permute-start.2 = (bf16[64,512]{1,0:T(8,128)(2,1)S(1)}, bf16[64,512]{1,0:T(8,128)(2,1)S(1)}, u32[]{:S(2)}, u32[]{:S(2)}) collective-permute-start(bf16[64,512]{1,0:T(8,128)(2,1)S(1)} %constant_dynamic-slice_fusion.4), channel_id=1, source_target_pairs={{0,256},{16,272},{32,288},{48,304},{64,320},{80,336},{96,352},{112... | collective-permute-start | bytes 196616 | tf_op jit(solution)/shard_map/ppermute | solution.py:30
  247.8 2.2 collective-permute-done.2
  250.0 7.1 %collective-permute-start.3 = (bf16[32,512]{1,0:T(8,128)(2,1)S(1)}, bf16[32,512]{1,0:T(8,128)(2,1)S(1)}, u32[]{:S(2)}, u32[]{:S(2)}) collective-permute-start(bf16[32,512]{1,0:T(8,128)(2,1)S(1)} %constant_dynamic-slice_fusion.3), channel_id=1, source_target_pairs={{0,128},{16,144},{32,160},{48,176},{64,192},{80,208},{96,224},{112... | collective-permute-start | bytes 98312 | tf_op jit(solution)/shard_map/ppermute | solution.py:30
  257.1 1.5 collective-permute-done.3
  258.6 4.4 %collective-permute-start.4 = (bf16[16,512]{1,0:T(8,128)(2,1)S(1)}, bf16[16,512]{1,0:T(8,128)(2,1)S(1)}, u32[]{:S(2)}, u32[]{:S(2)}) collective-permute-start(bf16[16,512]{1,0:T(8,128)(2,1)S(1)} %constant_dynamic-slice_fusion.2), channel_id=1, source_target_pairs={{0,64},{16,80},{32,96},{48,112},{64,0},{80,16},{96,32},{112,48},{1... | collective-permute-start | bytes 49160 | tf_op jit(solution)/shard_map/ppermute | solution.py:30
  263.1 1.1 collective-permute-done.4
  264.2 2.9 %collective-permute-start.5 = (bf16[8,512]{1,0:T(8,128)(2,1)S(1)}, bf16[8,512]{1,0:T(8,128)(2,1)S(1)}, u32[]{:S(2)}, u32[]{:S(2)}) collective-permute-start(bf16[8,512]{1,0:T(8,128)(2,1)S(1)} %constant_dynamic-slice_fusion.1), channel_id=1, source_target_pairs={{0,32},{16,48},{32,0},{48,16},{64,96},{80,112},{96,64},{112,80},{1... | collective-permute-start | bytes 24584 | tf_op jit(solution)/shard_map/ppermute | solution.py:30
  267.2 1.4 collective-permute-done.5
  268.6 7.0 %collective-permute-start.6 = (bf16[4,512]{1,0:T(4,128)(2,1)S(1)}, bf16[4,512]{1,0:T(4,128)(2,1)S(1)}, u32[]{:S(2)}, u32[]{:S(2)}) collective-permute-start(bf16[4,512]{1,0:T(4,128)(2,1)S(1)} %constant_dynamic-slice_fusion), channel_id=1, source_target_pairs={{0,16},{16,0},{32,48},{48,32},{64,80},{80,64},{96,112},{112,96},{1... | collective-permute-start | bytes 12296 | tf_op jit(solution)/shard_map/ppermute | solution.py:30
  (38 shorter events, 7.3 us)
Async XLA Ops:
  7.2 123.5 %all-gather.2.cloned.1.call-start = ((), (), s32[]{:S(2)}) async-start(), calls=%async_computation.2 | async-start | bytes 8650752 | tf_op jit(solution)/shard_map/all_gather | solution.py:80
  7.9 207.5 %reduce-scatter.3.cloned.1.call-start = ((), (), s32[]{:S(2)}) async-start(), calls=%async_computation.3 | async-start | bytes 7077888 | tf_op jit(solution)/shard_map/reduce_scatter | solution.py:83
  8.7 58.8 %collective-permute-start = (bf16[3,2,512]{2,1,0:T(2,128)(2,1)S(1)}, bf16[3,2,512]{2,1,0:T(2,128)(2,1)S(1)}, u32[]{:S(2)}, u32[]{:S(2)}) collective-permute-start(bf16[3,2,512]{2,1,0:T(2,128)(2,1)S(1)} %slice.38), channel_id=1, source_target_pairs={{0,16},{16,32},{32,48},{48,64},{64,80},{80,96},{96,112},{112,128},... | collective-permute-start | bytes 18440 | tf_op jit(solution)/shard_map/ppermute | solution.py:15
  38.2 29.9 %copy-start = (bf16[3,384,512]{2,1,0:T(8,128)(2,1)S(1)}, bf16[3,384,512]{2,1,0:T(8,128)(2,1)}, u32[]{:S(2)}) copy-start(bf16[3,384,512]{2,1,0:T(8,128)(2,1)} %param.6) | copy-start | bytes 3538948
  67.5 0.6 copy-start.1
  69.8 5.7 %collective-permute-start.1 = (bf16[127,512]{1,0:T(8,128)(2,1)S(1)}, bf16[127,512]{1,0:T(8,128)(2,1)S(1)}, u32[]{:S(2)}, u32[]{:S(2)}) collective-permute-start(bf16[127,512]{1,0:T(8,128)(2,1)S(1)} %slice_bitcast_fusion.1), channel_id=1, source_target_pairs={{0,16},{16,32},{32,48},{48,64},{64,80},{80,96},{96,112},{112,128},... | collective-permute-start | bytes 390152 | tf_op jit(solution)/shard_map/ppermute | solution.py:15
  76.6 54.1 %copy-start.2 = (f32[512]{0:T(512)S(1)}, f32[512]{0:T(512)}, u32[]{:S(2)}) copy-start(f32[512]{0:T(512)} %param.9) | copy-start | bytes 6148
  140.5 75.0 %copy-start.3 = (s32[128]{0:T(128)S(1)}, s32[128]{0:T(128)}, u32[]{:S(2)}) copy-start(s32[128]{0:T(128)} %param.11) | copy-start | bytes 1540
  140.5 101.7 %reduce-scatter.5.cloned.1.call-start = ((), (), s32[]{:S(2)}) async-start(), calls=%async_computation.4 | async-start | bytes 1179648 | tf_op jit(solution)/shard_map/reduce_scatter | solution.py:84
  243.5 6.5 %collective-permute-start.2 = (bf16[64,512]{1,0:T(8,128)(2,1)S(1)}, bf16[64,512]{1,0:T(8,128)(2,1)S(1)}, u32[]{:S(2)}, u32[]{:S(2)}) collective-permute-start(bf16[64,512]{1,0:T(8,128)(2,1)S(1)} %constant_dynamic-slice_fusion.4), channel_id=1, source_target_pairs={{0,256},{16,272},{32,288},{48,304},{64,320},{80,336},{96,352},{112... | collective-permute-start | bytes 196616 | tf_op jit(solution)/shard_map/ppermute | solution.py:30
  250.0 8.6 %collective-permute-start.3 = (bf16[32,512]{1,0:T(8,128)(2,1)S(1)}, bf16[32,512]{1,0:T(8,128)(2,1)S(1)}, u32[]{:S(2)}, u32[]{:S(2)}) collective-permute-start(bf16[32,512]{1,0:T(8,128)(2,1)S(1)} %constant_dynamic-slice_fusion.3), channel_id=1, source_target_pairs={{0,128},{16,144},{32,160},{48,176},{64,192},{80,208},{96,224},{112... | collective-permute-start | bytes 98312 | tf_op jit(solution)/shard_map/ppermute | solution.py:30
  258.6 5.5 %collective-permute-start.4 = (bf16[16,512]{1,0:T(8,128)(2,1)S(1)}, bf16[16,512]{1,0:T(8,128)(2,1)S(1)}, u32[]{:S(2)}, u32[]{:S(2)}) collective-permute-start(bf16[16,512]{1,0:T(8,128)(2,1)S(1)} %constant_dynamic-slice_fusion.2), channel_id=1, source_target_pairs={{0,64},{16,80},{32,96},{48,112},{64,0},{80,16},{96,32},{112,48},{1... | collective-permute-start | bytes 49160 | tf_op jit(solution)/shard_map/ppermute | solution.py:30
  264.2 4.4 %collective-permute-start.5 = (bf16[8,512]{1,0:T(8,128)(2,1)S(1)}, bf16[8,512]{1,0:T(8,128)(2,1)S(1)}, u32[]{:S(2)}, u32[]{:S(2)}) collective-permute-start(bf16[8,512]{1,0:T(8,128)(2,1)S(1)} %constant_dynamic-slice_fusion.1), channel_id=1, source_target_pairs={{0,32},{16,48},{32,0},{48,16},{64,96},{80,112},{96,64},{112,80},{1... | collective-permute-start | bytes 24584 | tf_op jit(solution)/shard_map/ppermute | solution.py:30
  268.6 7.8 %collective-permute-start.6 = (bf16[4,512]{1,0:T(4,128)(2,1)S(1)}, bf16[4,512]{1,0:T(4,128)(2,1)S(1)}, u32[]{:S(2)}, u32[]{:S(2)}) collective-permute-start(bf16[4,512]{1,0:T(4,128)(2,1)S(1)} %constant_dynamic-slice_fusion), channel_id=1, source_target_pairs={{0,16},{16,0},{32,48},{48,32},{64,80},{80,64},{96,112},{112,96},{1... | collective-permute-start | bytes 12296 | tf_op jit(solution)/shard_map/ppermute | solution.py:30
Sparse Core Ops, SparseCore 0:
  11.1 119.4 all-gather.1
  140.6 74.7 reduce-scatter.2
  218.8 23.3 reduce-scatter.4

commit v3 on v2

--- a/solution.py
+++ b/solution.py
@@ -15,21 +15,20 @@
     return lax.ppermute(array, axis, pairs)
 
 
-def halving_scatter(rows, axis):
+def pair_scatter(block, axis):
+    me = lax.axis_index(axis)
+    half = block.shape[1] // 2
+    keep = lax.dynamic_slice_in_dim(block, me * half, half, 1)
+    send = lax.dynamic_slice_in_dim(block, (1 - me) * half, half, 1)
+    got = lax.ppermute(send, axis, [(0, 1), (1, 0)])
+    return (keep.astype(jnp.float32) + got.astype(jnp.float32)).astype(block.dtype)
+
+
+def exchange_scatter(rows, axis):
     size = lax.axis_size(axis)
-    if size & (size - 1) or rows.shape[0] % size:
-        return lax.psum_scatter(rows, axis, scatter_dimension=0, tiled=True)
-    me = lax.axis_index(axis)
-    step = size // 2
-    while step >= 1:
-        half = rows.shape[0] // 2
-        bit = (me // step) % 2
-        keep = lax.dynamic_slice_in_dim(rows, bit * half, half, 0)
-        send = lax.dynamic_slice_in_dim(rows, (1 - bit) * half, half, 0)
-        pairs = [(i, i ^ step) for i in range(size)]
-        rows = keep + lax.ppermute(send, axis, pairs)
-        step //= 2
-    return rows
+    pieces = rows.reshape(size, rows.shape[0] // size, rows.shape[1])
+    pieces = lax.all_to_all(pieces, axis, 0, 0, tiled=True)
+    return pieces.astype(jnp.float32).sum(0).astype(rows.dtype)
 
 
 def short_filter(extended, weights, count):
@@ -81,14 +80,14 @@
         preferred_element_type=jnp.float32,
     )
     mixed = lax.psum_scatter(terms.astype(jnp.bfloat16), "z", scatter_dimension=1, tiled=True)
-    mixed = lax.psum_scatter(mixed, "x_lo", scatter_dimension=1, tiled=True)
+    mixed = pair_scatter(mixed, "x_lo")
     offset = lax.axis_index("context") * rows
     local_sites = positions - offset
     one_hot = (local_sites[:, None] == jnp.arange(rows, dtype=jnp.int32)[None, :]).astype(
         jnp.bfloat16
     )
     picked_terms = jnp.dot(one_hot, mixed, preferred_element_type=jnp.float32)
-    variant_states = halving_scatter(picked_terms.astype(jnp.bfloat16), "context")
+    variant_states = exchange_scatter(picked_terms.astype(jnp.bfloat16), "context")
     return (mixed, variant_states)
 
 

time: 284 us -> 259 us (0.912)
  waiting for transfers between devices: 157 us -> 133 us
  starting transfers between devices: 32.6 us -> 9.86 us
  blocking collectives: 0 us -> 21.1 us
    reduce_scatter x1 -> x0, waiting for transfers between devices: 26.7 us -> none  [on_device(): mixed = lax.psum_scatter(mixed, 'x_lo', scatter_dimension=1, tiled=True)]
    ppermute x5 -> x1, starting transfers between devices: 25.8 us -> 3.09 us  [pair_scatter(): got = lax.ppermute(send, axis, [(0, 1), (1, 0)])]
    all_to_all x0 -> x1, blocking collectives: none -> 21.1 us  [exchange_scatter(): pieces = lax.all_to_all(pieces, axis, 0, 0, tiled=True)]
    ppermute x5 -> x1, waiting for transfers between devices: 6.9 us -> 8.82 us  [pair_scatter(): got = lax.ppermute(send, axis, [(0, 1), (1, 0)])]
    unnamed x11 -> x13, local copies, waits for them, and re-layouts: 13.2 us -> 13.2 us
  transfers between devices with their start and end apart: 10 -> 5, of which waited for: 9 -> 4; matrix products, arithmetic and copies ran while one was open for 24% -> 26% of each run, Pallas kernels for 0% -> 0%
where the time goes in v3:
time: 259 us; the launch traced here: 258 us
  waiting for transfers between devices  133 us (51%)
  local copies, waits for them, and re-layouts  58.8 us (23%)
  blocking collectives  21.1 us (8%)
  matrix products  18.4 us (7%)
  between operations  14.2 us (5%)
  starting transfers between devices  9.86 us (4%)
  other arithmetic  3.62 us (1%)
    reduce_scatter x1, waiting for transfers between devices, on_device(): lax.psum_scatter(terms.astype(jnp.bfloat16), 'z', scatter_dimension=1, ti...  74.9 us
    all_gather x1, waiting for transfers between devices, on_device(): lax.all_gather(out_weight, 'context', axis=1, tiled=True)  44.6 us
    reshape x1, local copies, waits for them, and re-layouts, banded_filters(): return tiled[:, :rows * span].reshape(local_groups, rows, span)  29.3 us
    all_to_all x1, blocking collectives, exchange_scatter(): pieces = lax.all_to_all(pieces, axis, 0, 0, tiled=True)  21.1 us
    unnamed x13, local copies, waits for them, and re-layouts  13.2 us
    dot_general x1, matrix products, on_device(): jnp.dot(gated, lax.all_gather(out_weight, 'context', axis=1, tiled=True),...  9.77 us
    ppermute x1, waiting for transfers between devices, pair_scatter(): got = lax.ppermute(send, axis, [(0, 1), (1, 0)])  8.82 us
    dot_general x1, matrix products, on_device(): jnp.einsum('gim,mgc->igc', toeplitz, extended.reshape(span, local_groups,...  8.33 us
  transfers between devices with their start and end apart: 5, of which 4 were waited for; matrix products, arithmetic and copies ran while one was open for 26% of the time, Pallas kernels for 0%

profile of v3, /device:TPU:1, one launch (start us, length us, event | category | flops | bytes accessed | tf_op | source)
XLA Modules:
  0.0 258.5 jit_solution(2116520121781968576)
XLA Ops:
  7.2 0.7 all-gather.2.cloned.1.call-update
  7.9 0.8 slice.38
  8.7 4.6 %collective-permute-start = (bf16[3,2,512]{2,1,0:T(2,128)(2,1)S(1)}, bf16[3,2,512]{2,1,0:T(2,128)(2,1)S(1)}, u32[]{:S(2)}, u32[]{:S(2)}) collective-permute-start(bf16[3,2,512]{2,1,0:T(2,128)(2,1)S(1)} %slice.38), channel_id=1, source_target_pairs={{0,16},{16,32},{32,48},{48,64},{64,80},{80,96},{96,112},{112,128},... | collective-permute-start | bytes 18440 | tf_op jit(solution)/shard_map/ppermute | solution.py:15
  13.3 0.9 fusion.8
  14.8 0.8 rev.4
  15.6 5.4 %tile.4 = bf16[32,384,512]{2,1,0:T(8,128)(2,1)} broadcast(bf16[32,512]{1,0:T(8,128)(2,1)S(1)} %concatenate.11), dimensions={0,2} | broadcast | bytes 12615680 | tf_op jit(solution)/shard_map/tile | solution.py:51
  21.0 12.0 %copy.15 = bf16[4,8,384,512]{3,1,2,0:T(8,128)(2,1)S(1)} copy(bf16[4,8,384,512]{3,2,1,0:T(8,128)(2,1)} %bitcast.32) | data formatting | bytes 25165824
  33.0 5.1 %slice.54 = bf16[32,196224]{1,0:T(8,128)(2,1)} slice(bf16[32,196608]{1,0:T(8,128)(2,1)S(1)} %bitcast.33), slice={[0:32], [0:196224]} | slice | bytes 25116672 | tf_op jit(solution)/shard_map/slice | solution.py:52
  38.2 29.3 %reshape.26 = bf16[32,384,511]{2,1,0:T(8,128)(2,1)} reshape(bf16[32,196224]{1,0:T(8,128)(2,1)} %slice.54) | data formatting | bytes 25116672 | tf_op jit(solution)/shard_map/reshape | solution.py:52
  68.0 1.5 multiply_add_fusion
  69.7 2.1 collective-permute-start.1
  72.0 3.5 %collective-permute-done.1 = bf16[127,512]{1,0:T(8,128)(2,1)S(1)} collective-permute-done((bf16[127,512]{1,0:T(8,128)(2,1)S(1)}, bf16[127,512]{1,0:T(8,128)(2,1)S(1)}, u32[]{:S(2)}, u32[]{:S(2)}) %collective-permute-start.1) | collective-permute-done | bytes 130080 | tf_op jit(solution)/shard_map/ppermute | solution.py:15
  75.5 1.0 copy.10
  76.6 8.3 %fusion.9 = f32[32,16,384]{2,1,0:T(8,128)S(1)} fusion(bf16[511,32,16]{0,2,1:T(8,128)(2,1)} %bitcast.35, bf16[32,384,511]{2,1,0:T(8,128)(2,1)} %reshape.26), kind=kOutput, calls=%fused_computation.25 | convolution fusion | flops 200933376 | bytes 13868032 | tf_op jit(solution)/shard_map/gim,mgc->igc/dot_general | solution.py:69
  84.9 1.2 copy.11
  86.1 44.6 %all-gather.2.cloned.1.call-done = bf16[512,8192]{1,0:T(8,128)(2,1)} async-done(((bf16[512,256]{1,0:T(8,128)(2,1)}), bf16[512,8192]{1,0:T(8,128)(2,1)}) %all-gather.2.cloned.1.call-update) | async-done | bytes 8388624 | tf_op jit(solution)/shard_map/all_gather | solution.py:79
  130.7 9.8 %convolution_convert_fusion = bf16[384,8192]{1,0:T(8,128)(2,1)} fusion(bf16[512,8192]{1,0:T(8,128)(2,1)} %all-gather.2.cloned.1.call-done, f32[3,384,512]{2,1,0:T(8,128)S(1)} %multiply_add_fusion, f32[384,512]{1,0:T(8,128)} %copy.11, f32[512]{0:T(512)S(1)} %copy-done.3, bf16[1,384,512]{2,1,0:T(8,128)(2,1)S(1)} %fusion.1), kind=kOutput, calls=%fused_computation | convolution fusion | flops 3225354240 | bytes 16648192 | tf_op jit(solution)/shard_map/dot_general | solution.py:77
  140.5 74.9 %reduce-scatter.2.cloned.1.call-done = bf16[384,1024]{1,0:T(8,128)(2,1)} async-done(((bf16[384,8192]{1,0:T(8,128)(2,1)}), bf16[384,1024]{1,0:T(8,128)(2,1)}) %reduce-scatter.2.cloned.1.call-update) | async-done | bytes 786448 | tf_op jit(solution)/shard_map/reduce_scatter | solution.py:82
  215.4 1.0 constant_dynamic-slice_fusion
  216.4 3.1 %collective-permute-start.2 = (bf16[384,512]{1,0:T(8,128)(2,1)S(1)}, bf16[384,512]{1,0:T(8,128)(2,1)S(1)}, u32[]{:S(2)}, u32[]{:S(2)}) collective-permute-start(bf16[384,512]{1,0:T(8,128)(2,1)S(1)} %constant_dynamic-slice_fusion), channel_id=1, source_target_pairs={{0,1},{1,0},{2,3},{3,2},{4,5},{5,4},{6,7},{7,6},{8,9},{9,8},{10,11... | collective-permute-start | bytes 1179656 | tf_op jit(solution)/shard_map/ppermute | solution.py:23
  219.6 8.8 %collective-permute-done.2 = bf16[384,512]{1,0:T(8,128)(2,1)S(1)} collective-permute-done((bf16[384,512]{1,0:T(8,128)(2,1)S(1)}, bf16[384,512]{1,0:T(8,128)(2,1)S(1)}, u32[]{:S(2)}, u32[]{:S(2)}) %collective-permute-start.2) | collective-permute-done | bytes 393248 | tf_op jit(solution)/shard_map/ppermute | solution.py:23
  228.4 1.1 add_convert_fusion
  229.8 21.1 %all_to_all.5 = bf16[32,4,512]{2,1,0:T(4,128)(2,1)S(1)} all-to-all(bf16[32,4,512]{2,1,0:T(4,128)(2,1)S(1)} %reshape.28), channel_id=1, replica_groups=mesh['context'=32,'z'=8,'x_lo'=2] {'context'}, dimensions={0} | all-to-all | bytes 262144 | tf_op jit(solution)/shard_map/all_to_all | solution.py:30
  250.9 0.7 reduce_sum.12
  (24 shorter events, 2.0 us)
Async XLA Ops:
  7.2 123.5 %all-gather.2.cloned.1.call-start = ((), (), s32[]{:S(2)}) async-start(), calls=%async_computation.2 | async-start | bytes 8650752 | tf_op jit(solution)/shard_map/all_gather | solution.py:79
  7.9 207.5 %reduce-scatter.2.cloned.1.call-start = ((), (), s32[]{:S(2)}) async-start(), calls=%async_computation.3 | async-start | bytes 7077888 | tf_op jit(solution)/shard_map/reduce_scatter | solution.py:82
  8.7 58.8 %collective-permute-start = (bf16[3,2,512]{2,1,0:T(2,128)(2,1)S(1)}, bf16[3,2,512]{2,1,0:T(2,128)(2,1)S(1)}, u32[]{:S(2)}, u32[]{:S(2)}) collective-permute-start(bf16[3,2,512]{2,1,0:T(2,128)(2,1)S(1)} %slice.38), channel_id=1, source_target_pairs={{0,16},{16,32},{32,48},{48,64},{64,80},{80,96},{96,112},{112,128},... | collective-permute-start | bytes 18440 | tf_op jit(solution)/shard_map/ppermute | solution.py:15
  38.2 29.9 %copy-start.1 = (bf16[3,384,512]{2,1,0:T(8,128)(2,1)S(1)}, bf16[3,384,512]{2,1,0:T(8,128)(2,1)}, u32[]{:S(2)}) copy-start(bf16[3,384,512]{2,1,0:T(8,128)(2,1)} %param.6) | copy-start | bytes 3538948
  67.4 0.6 copy-start.2
  69.7 5.7 %collective-permute-start.1 = (bf16[127,512]{1,0:T(8,128)(2,1)S(1)}, bf16[127,512]{1,0:T(8,128)(2,1)S(1)}, u32[]{:S(2)}, u32[]{:S(2)}) collective-permute-start(bf16[127,512]{1,0:T(8,128)(2,1)S(1)} %slice_bitcast_fusion.1), channel_id=1, source_target_pairs={{0,16},{16,32},{32,48},{48,64},{64,80},{80,96},{96,112},{112,128},... | collective-permute-start | bytes 390152 | tf_op jit(solution)/shard_map/ppermute | solution.py:15
  76.6 54.1 %copy-start.3 = (f32[512]{0:T(512)S(1)}, f32[512]{0:T(512)}, u32[]{:S(2)}) copy-start(f32[512]{0:T(512)} %param.9) | copy-start | bytes 6148
  140.5 79.1 %copy-start.4 = (s32[128]{0:T(128)S(1)}, s32[128]{0:T(128)}, u32[]{:S(2)}) copy-start(s32[128]{0:T(128)} %param.11) | copy-start | bytes 1540
  216.4 11.9 %collective-permute-start.2 = (bf16[384,512]{1,0:T(8,128)(2,1)S(1)}, bf16[384,512]{1,0:T(8,128)(2,1)S(1)}, u32[]{:S(2)}, u32[]{:S(2)}) collective-permute-start(bf16[384,512]{1,0:T(8,128)(2,1)S(1)} %constant_dynamic-slice_fusion), channel_id=1, source_target_pairs={{0,1},{1,0},{2,3},{3,2},{4,5},{5,4},{6,7},{7,6},{8,9},{9,8},{10,11... | collective-permute-start | bytes 1179656 | tf_op jit(solution)/shard_map/ppermute | solution.py:23
  229.5 22.1 %copy-start = (bf16[384,512]{1,0:T(8,128)(2,1)}, bf16[384,512]{1,0:T(8,128)(2,1)S(1)}, u32[]{:S(2)}) copy-start(bf16[384,512]{1,0:T(8,128)(2,1)S(1)} %add_convert_fusion) | copy-start | bytes 1179652
Sparse Core Ops, SparseCore 0:
  11.1 119.4 all-gather.1
  140.6 74.7 reduce-scatter.1

commit v4 on v3

--- a/solution.py
+++ b/solution.py
@@ -79,15 +79,16 @@
         lax.all_gather(out_weight, "context", axis=1, tiled=True),
         preferred_element_type=jnp.float32,
     )
-    mixed = lax.psum_scatter(terms.astype(jnp.bfloat16), "z", scatter_dimension=1, tiled=True)
-    mixed = pair_scatter(mixed, "x_lo")
+    partial = lax.psum_scatter(terms.astype(jnp.bfloat16), "z", scatter_dimension=1, tiled=True)
+    mixed = pair_scatter(partial, "x_lo")
     offset = lax.axis_index("context") * rows
     local_sites = positions - offset
     one_hot = (local_sites[:, None] == jnp.arange(rows, dtype=jnp.int32)[None, :]).astype(
         jnp.bfloat16
     )
-    picked_terms = jnp.dot(one_hot, mixed, preferred_element_type=jnp.float32)
-    variant_states = exchange_scatter(picked_terms.astype(jnp.bfloat16), "context")
+    picked_terms = jnp.dot(one_hot, partial, preferred_element_type=jnp.float32)
+    picked = exchange_scatter(picked_terms.astype(jnp.bfloat16), "context")
+    variant_states = pair_scatter(picked, "x_lo")
     return (mixed, variant_states)
 
 

time: 259 us -> 254 us (0.981)
  blocking collectives: 21.1 us -> 0 us
  starting transfers between devices: 9.86 us -> 21.1 us
    all_to_all x1 -> x0, blocking collectives: 21.1 us -> none  [exchange_scatter(): pieces = lax.all_to_all(pieces, axis, 0, 0, tiled=True)]
    all_to_all x0 -> x1, waiting for transfers between devices: none -> 11.1 us  [exchange_scatter(): pieces = lax.all_to_all(pieces, axis, 0, 0, tiled=True)]
    all_to_all x0 -> x1, starting transfers between devices: none -> 9.92 us  [exchange_scatter(): pieces = lax.all_to_all(pieces, axis, 0, 0, tiled=True)]
    ppermute x1 -> x2, waiting for transfers between devices: 8.82 us -> 1.26 us  [pair_scatter(): got = lax.ppermute(send, axis, [(0, 1), (1, 0)])]
  transfers between devices with their start and end apart: 5 -> 7, of which waited for: 4 -> 5; matrix products, arithmetic and copies ran while one was open for 26% -> 27% of each run, Pallas kernels for 0% -> 0%
where the time goes in v4:
time: 254 us; the launch traced here: 253 us
  waiting for transfers between devices  135 us (53%)
  local copies, waits for them, and re-layouts  59.1 us (23%)
  starting transfers between devices  21.1 us (8%)
  matrix products  19.6 us (8%)
  between operations  14.2 us (6%)
  other arithmetic  3.45 us (1%)
    reduce_scatter x1, waiting for transfers between devices, on_device(): lax.psum_scatter(terms.astype(jnp.bfloat16), 'z', scatter_dimension=1, ti...  74.3 us
    all_gather x1, waiting for transfers between devices, on_device(): lax.all_gather(out_weight, 'context', axis=1, tiled=True)  44.6 us
    reshape x1, local copies, waits for them, and re-layouts, banded_filters(): return tiled[:, :rows * span].reshape(local_groups, rows, span)  29.3 us
    unnamed x13, local copies, waits for them, and re-layouts  13.9 us
    all_to_all x1, waiting for transfers between devices, exchange_scatter(): pieces = lax.all_to_all(pieces, axis, 0, 0, tiled=True)  11.1 us
    all_to_all x1, starting transfers between devices, exchange_scatter(): pieces = lax.all_to_all(pieces, axis, 0, 0, tiled=True)  9.92 us
    dot_general x1, matrix products, on_device(): jnp.dot(gated, lax.all_gather(out_weight, 'context', axis=1, tiled=True),...  9.76 us
    dot_general x1, matrix products, on_device(): jnp.einsum('gim,mgc->igc', toeplitz, extended.reshape(span, local_groups,...  8.33 us
  transfers between devices with their start and end apart: 7, of which 5 were waited for; matrix products, arithmetic and copies ran while one was open for 27% of the time, Pallas kernels for 0%

profile of v4, /device:TPU:1, one launch (start us, length us, event | category | flops | bytes accessed | tf_op | source)
XLA Modules:
  0.0 253.0 jit_solution(7069590457297672388)
XLA Ops:
  8.7 4.6 %collective-permute-start = (bf16[3,2,512]{2,1,0:T(2,128)(2,1)S(1)}, bf16[3,2,512]{2,1,0:T(2,128)(2,1)S(1)}, u32[]{:S(2)}, u32[]{:S(2)}) collective-permute-start(bf16[3,2,512]{2,1,0:T(2,128)(2,1)S(1)} %slice.38), channel_id=1, source_target_pairs={{0,16},{16,32},{32,48},{48,64},{64,80},{80,96},{96,112},{112,128},... | collective-permute-start | bytes 18440 | tf_op jit(solution)/shard_map/ppermute | solution.py:15
  13.3 0.9 fusion.8
  14.8 0.8 rev.4
  15.6 5.4 %tile.4 = bf16[32,384,512]{2,1,0:T(8,128)(2,1)} broadcast(bf16[32,512]{1,0:T(8,128)(2,1)S(1)} %concatenate.11), dimensions={0,2} | broadcast | bytes 12615680 | tf_op jit(solution)/shard_map/tile | solution.py:51
  21.0 12.0 %copy.15 = bf16[4,8,384,512]{3,1,2,0:T(8,128)(2,1)S(1)} copy(bf16[4,8,384,512]{3,2,1,0:T(8,128)(2,1)} %bitcast.32) | data formatting | bytes 25165824
  33.0 5.1 %slice.54 = bf16[32,196224]{1,0:T(8,128)(2,1)} slice(bf16[32,196608]{1,0:T(8,128)(2,1)S(1)} %bitcast.33), slice={[0:32], [0:196224]} | slice | bytes 25116672 | tf_op jit(solution)/shard_map/slice | solution.py:52
  38.1 29.3 %reshape.26 = bf16[32,384,511]{2,1,0:T(8,128)(2,1)} reshape(bf16[32,196224]{1,0:T(8,128)(2,1)} %slice.54) | data formatting | bytes 25116672 | tf_op jit(solution)/shard_map/reshape | solution.py:52
  68.0 1.5 multiply_add_fusion
  69.7 2.1 collective-permute-start.1
  72.0 3.5 %collective-permute-done.1 = bf16[127,512]{1,0:T(8,128)(2,1)S(1)} collective-permute-done((bf16[127,512]{1,0:T(8,128)(2,1)S(1)}, bf16[127,512]{1,0:T(8,128)(2,1)S(1)}, u32[]{:S(2)}, u32[]{:S(2)}) %collective-permute-start.1) | collective-permute-done | bytes 130080 | tf_op jit(solution)/shard_map/ppermute | solution.py:15
  75.5 1.0 copy.10
  76.5 8.3 %fusion.9 = f32[32,16,384]{2,1,0:T(8,128)S(1)} fusion(bf16[511,32,16]{0,2,1:T(8,128)(2,1)} %bitcast.35, bf16[32,384,511]{2,1,0:T(8,128)(2,1)} %reshape.26), kind=kOutput, calls=%fused_computation.27 | convolution fusion | flops 200933376 | bytes 13868032 | tf_op jit(solution)/shard_map/gim,mgc->igc/dot_general | solution.py:69
  84.9 1.2 copy.11
  86.0 44.6 %all-gather.2.cloned.1.call-done = bf16[512,8192]{1,0:T(8,128)(2,1)} async-done(((bf16[512,256]{1,0:T(8,128)(2,1)}), bf16[512,8192]{1,0:T(8,128)(2,1)}) %all-gather.2.cloned.1.call-update) | async-done | bytes 8388624 | tf_op jit(solution)/shard_map/all_gather | solution.py:79
  130.7 9.8 %convolution_convert_fusion = bf16[384,8192]{1,0:T(8,128)(2,1)} fusion(bf16[512,8192]{1,0:T(8,128)(2,1)} %all-gather.2.cloned.1.call-done, f32[3,384,512]{2,1,0:T(8,128)S(1)} %multiply_add_fusion, f32[384,512]{1,0:T(8,128)} %copy.11, f32[512]{0:T(512)S(1)} %copy-done.3, bf16[1,384,512]{2,1,0:T(8,128)(2,1)S(1)} %fusion.1), kind=kOutput, calls=%fused_computation | convolution fusion | flops 3225354240 | bytes 16648192 | tf_op jit(solution)/shard_map/dot_general | solution.py:77
  141.1 74.3 %reduce-scatter.2.cloned.1.call-done = bf16[384,1024]{1,0:T(8,128)(2,1)} async-done(((bf16[384,8192]{1,0:T(8,128)(2,1)}), bf16[384,1024]{1,0:T(8,128)(2,1)}) %reduce-scatter.2.cloned.1.call-update) | async-done | bytes 786448 | tf_op jit(solution)/shard_map/reduce_scatter | solution.py:82
  215.4 1.6 convolution_convert_fusion.1
  216.9 0.8 reshape.28
  217.7 9.9 %all-to-all-start = ((bf16[32,4,1024]{2,1,0:T(4,128)(2,1)}), bf16[32,4,1024]{2,1,0:T(4,128)(2,1)S(1)}, u32[]{:S(2)}, u32[]{:S(2)}) async-start(bf16[32,4,1024]{2,1,0:T(4,128)(2,1)} %reshape.28), calls=%async_computation.1 | async-start | bytes 524288 | tf_op jit(solution)/shard_map/all_to_all | solution.py:30
  227.7 2.2 collective-permute-start.2
  229.9 11.1 %all-to-all-done = bf16[32,4,1024]{2,1,0:T(4,128)(2,1)S(1)} async-done(((bf16[32,4,1024]{2,1,0:T(4,128)(2,1)}), bf16[32,4,1024]{2,1,0:T(4,128)(2,1)S(1)}, u32[]{:S(2)}, u32[]{:S(2)}) %all-to-all-start) | async-done | bytes 262176 | tf_op jit(solution)/shard_map/all_to_all | solution.py:30
  241.2 2.2 collective-permute-start.3
  243.4 0.9 add_convert_fusion
  244.3 1.3 collective-permute-done.3
  (29 shorter events, 4.5 us)
Async XLA Ops:
  7.2 123.5 %all-gather.2.cloned.1.call-start = ((), (), s32[]{:S(2)}) async-start(), calls=%async_computation.2 | async-start | bytes 8650752 | tf_op jit(solution)/shard_map/all_gather | solution.py:79
  7.9 207.5 %reduce-scatter.2.cloned.1.call-start = ((), (), s32[]{:S(2)}) async-start(), calls=%async_computation.3 | async-start | bytes 7077888 | tf_op jit(solution)/shard_map/reduce_scatter | solution.py:82
  8.7 58.7 %collective-permute-start = (bf16[3,2,512]{2,1,0:T(2,128)(2,1)S(1)}, bf16[3,2,512]{2,1,0:T(2,128)(2,1)S(1)}, u32[]{:S(2)}, u32[]{:S(2)}) collective-permute-start(bf16[3,2,512]{2,1,0:T(2,128)(2,1)S(1)} %slice.38), channel_id=1, source_target_pairs={{0,16},{16,32},{32,48},{48,64},{64,80},{80,96},{96,112},{112,128},... | collective-permute-start | bytes 18440 | tf_op jit(solution)/shard_map/ppermute | solution.py:15
  38.1 29.9 %copy-start.1 = (bf16[3,384,512]{2,1,0:T(8,128)(2,1)S(1)}, bf16[3,384,512]{2,1,0:T(8,128)(2,1)}, u32[]{:S(2)}) copy-start(bf16[3,384,512]{2,1,0:T(8,128)(2,1)} %param.6) | copy-start | bytes 3538948
  67.4 0.6 copy-start.2
  69.7 5.7 %collective-permute-start.1 = (bf16[127,512]{1,0:T(8,128)(2,1)S(1)}, bf16[127,512]{1,0:T(8,128)(2,1)S(1)}, u32[]{:S(2)}, u32[]{:S(2)}) collective-permute-start(bf16[127,512]{1,0:T(8,128)(2,1)S(1)} %slice_bitcast_fusion.1), channel_id=1, source_target_pairs={{0,16},{16,32},{32,48},{48,64},{64,80},{80,96},{96,112},{112,128},... | collective-permute-start | bytes 390152 | tf_op jit(solution)/shard_map/ppermute | solution.py:15
  76.5 54.2 %copy-start.3 = (f32[512]{0:T(512)S(1)}, f32[512]{0:T(512)}, u32[]{:S(2)}) copy-start(f32[512]{0:T(512)} %param.9) | copy-start | bytes 6148
  140.4 0.7 copy-start.4
  215.3 12.3 %copy-start = (bf16[384,1024]{1,0:T(8,128)(2,1)S(1)}, bf16[384,1024]{1,0:T(8,128)(2,1)}, u32[]{:S(2)}) copy-start(bf16[384,1024]{1,0:T(8,128)(2,1)} %reduce-scatter.2.cloned.1.call-done) | copy-start | bytes 2359300
  217.7 23.4 %all-to-all-start = ((bf16[32,4,1024]{2,1,0:T(4,128)(2,1)}), bf16[32,4,1024]{2,1,0:T(4,128)(2,1)S(1)}, u32[]{:S(2)}, u32[]{:S(2)}) async-start(bf16[32,4,1024]{2,1,0:T(4,128)(2,1)} %reshape.28), calls=%async_computation.1 | async-start | bytes 524288 | tf_op jit(solution)/shard_map/all_to_all | solution.py:30
  227.7 15.7 %collective-permute-start.2 = (bf16[384,512]{1,0:T(8,128)(2,1)S(1)}, bf16[384,512]{1,0:T(8,128)(2,1)S(1)}, u32[]{:S(2)}, u32[]{:S(2)}) collective-permute-start(bf16[384,512]{1,0:T(8,128)(2,1)S(1)} %constant_dynamic-slice_fusion.1), channel_id=1, source_target_pairs={{0,1},{1,0},{2,3},{3,2},{4,5},{5,4},{6,7},{7,6},{8,9},{9,8},{10,11... | collective-permute-start | bytes 1179656 | tf_op jit(solution)/shard_map/ppermute | solution.py:23
  241.2 4.4 %collective-permute-start.3 = (bf16[4,512]{1,0:T(4,128)(2,1)S(1)}, bf16[4,512]{1,0:T(4,128)(2,1)S(1)}, u32[]{:S(2)}, u32[]{:S(2)}) collective-permute-start(bf16[4,512]{1,0:T(4,128)(2,1)S(1)} %constant_dynamic-slice_fusion), channel_id=1, source_target_pairs={{0,1},{1,0},{2,3},{3,2},{4,5},{5,4},{6,7},{7,6},{8,9},{9,8},{10,11... | collective-permute-start | bytes 12296 | tf_op jit(solution)/shard_map/ppermute | solution.py:23
Sparse Core Ops, SparseCore 0:
  11.1 119.4 all-gather.1
  140.6 74.7 reduce-scatter.1

commit v5 on v4

--- a/solution.py
+++ b/solution.py
@@ -73,7 +73,7 @@
         preferred_element_type=jnp.float32,
     ).reshape(rows, width)
     conv = conv + skip[None, :] * product.astype(jnp.float32)
-    gated = (query * conv).astype(jnp.bfloat16)
+    gated = lax.optimization_barrier((query * conv).astype(jnp.bfloat16))
     terms = jnp.dot(
         gated,
         lax.all_gather(out_weight, "context", axis=1, tiled=True),

time: 254 us -> 253 us (level)
  no operation moved by 1% of the time
where the time goes in v5:
time: 253 us; the launch traced here: 252 us
  waiting for transfers between devices  135 us (53%)
  local copies, waits for them, and re-layouts  58.6 us (23%)
  starting transfers between devices  21.1 us (8%)
  matrix products  19.4 us (8%)
  between operations  14.2 us (6%)
  other arithmetic  3.83 us (2%)
    reduce_scatter x1, waiting for transfers between devices, on_device(): lax.psum_scatter(terms.astype(jnp.bfloat16), 'z', scatter_dimension=1, ti...  74.3 us
    all_gather x1, waiting for transfers between devices, on_device(): lax.all_gather(out_weight, 'context', axis=1, tiled=True)  44 us
    reshape x1, local copies, waits for them, and re-layouts, banded_filters(): return tiled[:, :rows * span].reshape(local_groups, rows, span)  29.3 us
    unnamed x13, local copies, waits for them, and re-layouts  13.9 us
    all_to_all x1, waiting for transfers between devices, exchange_scatter(): pieces = lax.all_to_all(pieces, axis, 0, 0, tiled=True)  11.1 us
    all_to_all x1, starting transfers between devices, exchange_scatter(): pieces = lax.all_to_all(pieces, axis, 0, 0, tiled=True)  9.92 us
    dot_general x1, matrix products, on_device(): jnp.einsum('gim,mgc->igc', toeplitz, extended.reshape(span, local_groups,...  9.07 us
    dot_general x1, matrix products, on_device(): jnp.dot(gated, lax.all_gather(out_weight, 'context', axis=1, tiled=True),...  8.74 us
  transfers between devices with their start and end apart: 7, of which 5 were waited for; matrix products, arithmetic and copies ran while one was open for 27% of the time, Pallas kernels for 0%

profile of v5, /device:TPU:1, one launch (start us, length us, event | category | flops | bytes accessed | tf_op | source)
XLA Modules:
  0.0 252.0 jit_solution(2760094707086557692)
XLA Ops:
  7.9 0.8 slice.38
  8.7 4.6 %collective-permute-start = (bf16[3,2,512]{2,1,0:T(2,128)(2,1)S(1)}, bf16[3,2,512]{2,1,0:T(2,128)(2,1)S(1)}, u32[]{:S(2)}, u32[]{:S(2)}) collective-permute-start(bf16[3,2,512]{2,1,0:T(2,128)(2,1)S(1)} %slice.38), channel_id=1, source_target_pairs={{0,16},{16,32},{32,48},{48,64},{64,80},{80,96},{96,112},{112,128},... | collective-permute-start | bytes 18440 | tf_op jit(solution)/shard_map/ppermute | solution.py:15
  13.3 0.9 fusion.5
  14.8 0.8 rev.4
  15.6 5.4 %tile.4 = bf16[32,384,512]{2,1,0:T(8,128)(2,1)} broadcast(bf16[32,512]{1,0:T(8,128)(2,1)S(1)} %concatenate.11), dimensions={0,2} | broadcast | bytes 12615680 | tf_op jit(solution)/shard_map/tile | solution.py:51
  21.0 12.0 %copy.15 = bf16[4,8,384,512]{3,1,2,0:T(8,128)(2,1)S(1)} copy(bf16[4,8,384,512]{3,2,1,0:T(8,128)(2,1)} %bitcast.29) | data formatting | bytes 25165824
  33.0 5.1 %slice.54 = bf16[32,196224]{1,0:T(8,128)(2,1)} slice(bf16[32,196608]{1,0:T(8,128)(2,1)S(1)} %bitcast.30), slice={[0:32], [0:196224]} | slice | bytes 25116672 | tf_op jit(solution)/shard_map/slice | solution.py:52
  38.1 29.3 %reshape.26 = bf16[32,384,511]{2,1,0:T(8,128)(2,1)} reshape(bf16[32,196224]{1,0:T(8,128)(2,1)} %slice.54) | data formatting | bytes 25116672 | tf_op jit(solution)/shard_map/reshape | solution.py:52
  68.0 1.5 multiply_add_fusion
  69.7 2.1 collective-permute-start.1
  72.0 3.5 %collective-permute-done.1 = bf16[127,512]{1,0:T(8,128)(2,1)S(1)} collective-permute-done((bf16[127,512]{1,0:T(8,128)(2,1)S(1)}, bf16[127,512]{1,0:T(8,128)(2,1)S(1)}, u32[]{:S(2)}, u32[]{:S(2)}) %collective-permute-start.1) | collective-permute-done | bytes 130080 | tf_op jit(solution)/shard_map/ppermute | solution.py:15
  75.8 9.1 %fusion.6 = f32[32,16,384]{2,1,0:T(8,128)} fusion(bf16[511,32,16]{0,2,1:T(8,128)(2,1)S(1)} %bitcast.32, bf16[32,384,511]{2,1,0:T(8,128)(2,1)} %reshape.26), kind=kOutput, calls=%fused_computation.25 | convolution fusion | flops 200933376 | bytes 13868032 | tf_op jit(solution)/shard_map/gim,mgc->igc/dot_general | solution.py:69
  84.8 1.4 copy.11
  86.6 44.0 %all-gather.2.cloned.1.call-done = bf16[512,8192]{1,0:T(8,128)(2,1)} async-done(((bf16[512,256]{1,0:T(8,128)(2,1)}), bf16[512,8192]{1,0:T(8,128)(2,1)}) %all-gather.2.cloned.1.call-update) | async-done | bytes 8388624 | tf_op jit(solution)/shard_map/all_gather | solution.py:79
  130.7 8.7 %convolution_convert_fusion = bf16[384,8192]{1,0:T(8,128)(2,1)} fusion(bf16[384,512]{1,0:T(8,128)(2,1)S(1)} %fusion.3, bf16[512,8192]{1,0:T(8,128)(2,1)} %all-gather.2.cloned.1.call-done), kind=kOutput, calls=%fused_computation | convolution fusion | flops 3224371200 | bytes 15073280 | tf_op jit(solution)/shard_map/dot_general | solution.py:77
  140.1 74.3 %reduce-scatter.2.cloned.1.call-done = bf16[384,1024]{1,0:T(8,128)(2,1)} async-done(((bf16[384,8192]{1,0:T(8,128)(2,1)}), bf16[384,1024]{1,0:T(8,128)(2,1)}) %reduce-scatter.2.cloned.1.call-update) | async-done | bytes 786448 | tf_op jit(solution)/shard_map/reduce_scatter | solution.py:82
  214.3 1.6 convolution_convert_fusion.1
  215.9 0.8 reshape.28
  216.7 9.9 %all-to-all-start = ((bf16[32,4,1024]{2,1,0:T(4,128)(2,1)}), bf16[32,4,1024]{2,1,0:T(4,128)(2,1)S(1)}, u32[]{:S(2)}, u32[]{:S(2)}) async-start(bf16[32,4,1024]{2,1,0:T(4,128)(2,1)} %reshape.28), calls=%async_computation.1 | async-start | bytes 524288 | tf_op jit(solution)/shard_map/all_to_all | solution.py:30
  226.7 2.2 collective-permute-start.2
  228.9 11.1 %all-to-all-done = bf16[32,4,1024]{2,1,0:T(4,128)(2,1)S(1)} async-done(((bf16[32,4,1024]{2,1,0:T(4,128)(2,1)}), bf16[32,4,1024]{2,1,0:T(4,128)(2,1)S(1)}, u32[]{:S(2)}, u32[]{:S(2)}) %all-to-all-start) | async-done | bytes 262176 | tf_op jit(solution)/shard_map/all_to_all | solution.py:30
  240.2 2.2 collective-permute-start.3
  242.4 0.9 add_convert_fusion
  243.3 1.2 collective-permute-done.3
  (30 shorter events, 4.3 us)
Async XLA Ops:
  7.2 123.5 %all-gather.2.cloned.1.call-start = ((), (), s32[]{:S(2)}) async-start(), calls=%async_computation.2 | async-start | bytes 8650752 | tf_op jit(solution)/shard_map/all_gather | solution.py:79
  7.9 206.4 %reduce-scatter.2.cloned.1.call-start = ((), (), s32[]{:S(2)}) async-start(), calls=%async_computation.3 | async-start | bytes 7077888 | tf_op jit(solution)/shard_map/reduce_scatter | solution.py:82
  8.7 58.7 %collective-permute-start = (bf16[3,2,512]{2,1,0:T(2,128)(2,1)S(1)}, bf16[3,2,512]{2,1,0:T(2,128)(2,1)S(1)}, u32[]{:S(2)}, u32[]{:S(2)}) collective-permute-start(bf16[3,2,512]{2,1,0:T(2,128)(2,1)S(1)} %slice.38), channel_id=1, source_target_pairs={{0,16},{16,32},{32,48},{48,64},{64,80},{80,96},{96,112},{112,128},... | collective-permute-start | bytes 18440 | tf_op jit(solution)/shard_map/ppermute | solution.py:15
  38.1 29.9 %copy-start.1 = (bf16[3,384,512]{2,1,0:T(8,128)(2,1)S(1)}, bf16[3,384,512]{2,1,0:T(8,128)(2,1)}, u32[]{:S(2)}) copy-start(bf16[3,384,512]{2,1,0:T(8,128)(2,1)} %param.6) | copy-start | bytes 3538948
  67.4 0.6 copy-start.2
  69.7 5.7 %collective-permute-start.1 = (bf16[127,512]{1,0:T(8,128)(2,1)S(1)}, bf16[127,512]{1,0:T(8,128)(2,1)S(1)}, u32[]{:S(2)}, u32[]{:S(2)}) collective-permute-start(bf16[127,512]{1,0:T(8,128)(2,1)S(1)} %slice_bitcast_fusion.1), channel_id=1, source_target_pairs={{0,16},{16,32},{32,48},{48,64},{64,80},{80,96},{96,112},{112,128},... | collective-permute-start | bytes 390152 | tf_op jit(solution)/shard_map/ppermute | solution.py:15
  75.7 10.5 %copy-start.3 = (f32[512]{0:T(512)S(1)}, f32[512]{0:T(512)}, u32[]{:S(2)}) copy-start(f32[512]{0:T(512)} %param.9) | copy-start | bytes 6148
  139.4 0.7 copy-start.4
  214.3 12.3 %copy-start = (bf16[384,1024]{1,0:T(8,128)(2,1)S(1)}, bf16[384,1024]{1,0:T(8,128)(2,1)}, u32[]{:S(2)}) copy-start(bf16[384,1024]{1,0:T(8,128)(2,1)} %reduce-scatter.2.cloned.1.call-done) | copy-start | bytes 2359300
  216.7 23.3 %all-to-all-start = ((bf16[32,4,1024]{2,1,0:T(4,128)(2,1)}), bf16[32,4,1024]{2,1,0:T(4,128)(2,1)S(1)}, u32[]{:S(2)}, u32[]{:S(2)}) async-start(bf16[32,4,1024]{2,1,0:T(4,128)(2,1)} %reshape.28), calls=%async_computation.1 | async-start | bytes 524288 | tf_op jit(solution)/shard_map/all_to_all | solution.py:30
  226.7 15.7 %collective-permute-start.2 = (bf16[384,512]{1,0:T(8,128)(2,1)S(1)}, bf16[384,512]{1,0:T(8,128)(2,1)S(1)}, u32[]{:S(2)}, u32[]{:S(2)}) collective-permute-start(bf16[384,512]{1,0:T(8,128)(2,1)S(1)} %constant_dynamic-slice_fusion.1), channel_id=1, source_target_pairs={{0,1},{1,0},{2,3},{3,2},{4,5},{5,4},{6,7},{7,6},{8,9},{9,8},{10,11... | collective-permute-start | bytes 1179656 | tf_op jit(solution)/shard_map/ppermute | solution.py:23
  240.2 4.4 %collective-permute-start.3 = (bf16[4,512]{1,0:T(4,128)(2,1)S(1)}, bf16[4,512]{1,0:T(4,128)(2,1)S(1)}, u32[]{:S(2)}, u32[]{:S(2)}) collective-permute-start(bf16[4,512]{1,0:T(4,128)(2,1)S(1)} %constant_dynamic-slice_fusion), channel_id=1, source_target_pairs={{0,1},{1,0},{2,3},{3,2},{4,5},{5,4},{6,7},{7,6},{8,9},{9,8},{10,11... | collective-permute-start | bytes 12296 | tf_op jit(solution)/shard_map/ppermute | solution.py:23
Sparse Core Ops, SparseCore 0:
  11.1 119.4 all-gather.1
  139.6 74.7 reduce-scatter.1

commit v6 on v5

--- a/solution.py
+++ b/solution.py
@@ -74,21 +74,24 @@
     ).reshape(rows, width)
     conv = conv + skip[None, :] * product.astype(jnp.float32)
     gated = lax.optimization_barrier((query * conv).astype(jnp.bfloat16))
-    terms = jnp.dot(
-        gated,
-        lax.all_gather(out_weight, "context", axis=1, tiled=True),
-        preferred_element_type=jnp.float32,
-    )
-    partial = lax.psum_scatter(terms.astype(jnp.bfloat16), "z", scatter_dimension=1, tiled=True)
-    mixed = pair_scatter(partial, "x_lo")
     offset = lax.axis_index("context") * rows
     local_sites = positions - offset
     one_hot = (local_sites[:, None] == jnp.arange(rows, dtype=jnp.int32)[None, :]).astype(
         jnp.bfloat16
     )
-    picked_terms = jnp.dot(one_hot, partial, preferred_element_type=jnp.float32)
-    picked = exchange_scatter(picked_terms.astype(jnp.bfloat16), "context")
-    variant_states = pair_scatter(picked, "x_lo")
+    picked_gated = jnp.dot(one_hot, gated, preferred_element_type=jnp.float32)
+    site_gated = exchange_scatter(picked_gated.astype(jnp.bfloat16), "context")
+    gated, site_gated = lax.optimization_barrier((gated, site_gated))
+    full_weight = lax.all_gather(out_weight, "context", axis=1, tiled=True)
+    terms = jnp.dot(gated, full_weight, preferred_element_type=jnp.float32)
+    partial = lax.psum_scatter(terms.astype(jnp.bfloat16), "z", scatter_dimension=1, tiled=True)
+    mixed = pair_scatter(partial, "x_lo")
+    site_terms = jnp.dot(site_gated, full_weight, preferred_element_type=jnp.float32)
+    site_terms = site_terms.astype(jnp.bfloat16)
+    blocks = lax.axis_size(("z", "x_lo"))
+    site_terms = site_terms.reshape(site_terms.shape[0], blocks, width).transpose(1, 0, 2)
+    site_terms = lax.all_to_all(site_terms, ("z", "x_lo"), 0, 0, tiled=True)
+    variant_states = site_terms.astype(jnp.float32).sum(0).astype(jnp.bfloat16)
     return (mixed, variant_states)
 
 

time: 253 us -> 250 us (0.988)
  waiting for transfers between devices: 135 us -> 110 us
  blocking collectives: 0 us -> 24.2 us
  starting transfers between devices: 21.1 us -> 14 us
  matrix products: 19.4 us -> 23.2 us
    all_to_all x0 -> x1, blocking collectives: none -> 24.2 us  [exchange_scatter(): pieces = lax.all_to_all(pieces, axis, 0, 0, tiled=True)]
    all_gather x1, waiting for transfers between devices: 44 us -> 20.6 us  [on_device(): full_weight = lax.all_gather(out_weight, 'context', axis=1, tiled=True)]
    all_to_all x1, starting transfers between devices: 9.92 us -> 3.99 us  [on_device(): site_terms = lax.all_to_all(site_terms, ('z', 'x_lo'), 0, 0, tiled=True)]
    dot_general x2 -> x3, matrix products: 10.3 us -> 14.2 us  [the longest x1 8.69 us: on_device(): terms = jnp.dot(gated, full_weight, preferred_element_type=jnp.float32)]
    all_to_all x1, waiting for transfers between devices: 11.1 us -> 7.89 us  [on_device(): site_terms = lax.all_to_all(site_terms, ('z', 'x_lo'), 0, 0, tiled=True)]
    reduce_scatter x1, waiting for transfers between devices: 74.3 us -> 77.2 us  [on_device(): lax.psum_scatter(terms.astype(jnp.bfloat16), 'z', scatter_dimension=1, ti...]
  transfers between devices with their start and end apart: 7 -> 6, of which waited for: 5 -> 4; matrix products, arithmetic and copies ran while one was open for 27% -> 30% of each run, Pallas kernels for 0% -> 0%
where the time goes in v6:
time: 250 us; the launch traced here: 249 us
  waiting for transfers between devices  110 us (44%)
  local copies, waits for them, and re-layouts  58.2 us (23%)
  blocking collectives  24.2 us (10%)
  matrix products  23.2 us (9%)
  between operations  14.2 us (6%)
  starting transfers between devices  14 us (6%)
  other arithmetic  4.99 us (2%)
    reduce_scatter x1, waiting for transfers between devices, on_device(): lax.psum_scatter(terms.astype(jnp.bfloat16), 'z', scatter_dimension=1, ti...  77.2 us
    reshape x1, local copies, waits for them, and re-layouts, banded_filters(): return tiled[:, :rows * span].reshape(local_groups, rows, span)  29.3 us
    all_to_all x1, blocking collectives, exchange_scatter(): pieces = lax.all_to_all(pieces, axis, 0, 0, tiled=True)  24.2 us
    all_gather x1, waiting for transfers between devices, on_device(): full_weight = lax.all_gather(out_weight, 'context', axis=1, tiled=True)  20.6 us
    unnamed x13, local copies, waits for them, and re-layouts  13.2 us
    dot_general x1, matrix products, on_device(): jnp.einsum('gim,mgc->igc', toeplitz, extended.reshape(span, local_groups,...  9.02 us
    dot_general x1, matrix products, on_device(): terms = jnp.dot(gated, full_weight, preferred_element_type=jnp.float32)  8.69 us
    all_to_all x1, waiting for transfers between devices, on_device(): site_terms = lax.all_to_all(site_terms, ('z', 'x_lo'), 0, 0, tiled=True)  7.89 us
  transfers between devices with their start and end apart: 6, of which 4 were waited for; matrix products, arithmetic and copies ran while one was open for 30% of the time, Pallas kernels for 0%

profile of v6, /device:TPU:1, one launch (start us, length us, event | category | flops | bytes accessed | tf_op | source)
XLA Modules:
  0.0 248.6 jit_solution(7654038640456595103)
XLA Ops:
  7.9 0.8 slice.38
  8.7 4.6 %collective-permute-start = (bf16[3,2,512]{2,1,0:T(2,128)(2,1)S(1)}, bf16[3,2,512]{2,1,0:T(2,128)(2,1)S(1)}, u32[]{:S(2)}, u32[]{:S(2)}) collective-permute-start(bf16[3,2,512]{2,1,0:T(2,128)(2,1)S(1)} %slice.38), channel_id=1, source_target_pairs={{0,16},{16,32},{32,48},{48,64},{64,80},{80,96},{96,112},{112,128},... | collective-permute-start | bytes 18440 | tf_op jit(solution)/shard_map/ppermute | solution.py:15
  13.3 0.9 fusion.5
  14.2 1.2 broadcast_subtract_fusion
  16.0 0.8 rev.4
  16.8 5.4 %tile.4 = bf16[32,384,512]{2,1,0:T(8,128)(2,1)} broadcast(bf16[32,512]{1,0:T(8,128)(2,1)S(1)} %concatenate.11), dimensions={0,2} | broadcast | bytes 12615680 | tf_op jit(solution)/shard_map/tile | solution.py:51
  22.2 12.0 %copy.18 = bf16[4,8,384,512]{3,1,2,0:T(8,128)(2,1)S(1)} copy(bf16[4,8,384,512]{3,2,1,0:T(8,128)(2,1)} %bitcast.34) | data formatting | bytes 25165824
  34.2 5.1 %slice.54 = bf16[32,196224]{1,0:T(8,128)(2,1)} slice(bf16[32,196608]{1,0:T(8,128)(2,1)S(1)} %bitcast.35), slice={[0:32], [0:196224]} | slice | bytes 25116672 | tf_op jit(solution)/shard_map/slice | solution.py:52
  39.3 29.3 %reshape.29 = bf16[32,384,511]{2,1,0:T(8,128)(2,1)} reshape(bf16[32,196224]{1,0:T(8,128)(2,1)} %slice.54) | data formatting | bytes 25116672 | tf_op jit(solution)/shard_map/reshape | solution.py:52
  69.2 1.5 multiply_add_fusion
  70.9 2.1 collective-permute-start.1
  73.1 3.4 %collective-permute-done.1 = bf16[127,512]{1,0:T(8,128)(2,1)S(1)} collective-permute-done((bf16[127,512]{1,0:T(8,128)(2,1)S(1)}, bf16[127,512]{1,0:T(8,128)(2,1)S(1)}, u32[]{:S(2)}, u32[]{:S(2)}) %collective-permute-start.1) | collective-permute-done | bytes 130080 | tf_op jit(solution)/shard_map/ppermute | solution.py:15
  76.9 9.0 %fusion.6 = f32[32,16,384]{2,1,0:T(8,128)} fusion(bf16[511,32,16]{0,2,1:T(8,128)(2,1)S(1)} %bitcast.37, bf16[32,384,511]{2,1,0:T(8,128)(2,1)} %reshape.29), kind=kOutput, calls=%fused_computation.24 | convolution fusion | flops 200933376 | bytes 13868032 | tf_op jit(solution)/shard_map/gim,mgc->igc/dot_general | solution.py:69
  85.9 1.4 copy.13
  88.1 24.2 %all_to_all.10 = bf16[32,4,512]{2,1,0:T(4,128)(2,1)S(1)} all-to-all(bf16[32,4,512]{2,1,0:T(4,128)(2,1)S(1)} %reshape.31), channel_id=1, replica_groups=mesh['context'=32,'z'=8,'x_lo'=2] {'context'}, dimensions={0} | all-to-all | bytes 262144 | tf_op jit(solution)/shard_map/all_to_all | solution.py:30
  112.3 20.6 %all-gather.2.cloned.1.call-done = bf16[512,8192]{1,0:T(8,128)(2,1)} async-done(((bf16[512,256]{1,0:T(8,128)(2,1)}), bf16[512,8192]{1,0:T(8,128)(2,1)}) %all-gather.2.cloned.1.call-update) | async-done | bytes 8388624 | tf_op jit(solution)/shard_map/all_gather | solution.py:85
  132.9 8.7 %convolution_convert_fusion = bf16[384,8192]{1,0:T(8,128)(2,1)} fusion(bf16[384,512]{1,0:T(8,128)(2,1)S(1)} %fusion.3, bf16[512,8192]{1,0:T(8,128)(2,1)} %all-gather.2.cloned.1.call-done), kind=kOutput, calls=%fused_computation | convolution fusion | flops 3224371200 | bytes 15073280 | tf_op jit(solution)/shard_map/dot_general | solution.py:86
  141.7 77.2 %reduce-scatter.2.cloned.1.call-done = bf16[384,1024]{1,0:T(8,128)(2,1)} async-done(((bf16[384,8192]{1,0:T(8,128)(2,1)}), bf16[384,1024]{1,0:T(8,128)(2,1)}) %reduce-scatter.2.cloned.1.call-update) | async-done | bytes 786448 | tf_op jit(solution)/shard_map/reduce_scatter | solution.py:87
  218.9 1.0 constant_dynamic-slice_fusion
  219.9 3.2 %collective-permute-start.2 = (bf16[384,512]{1,0:T(8,128)(2,1)S(1)}, bf16[384,512]{1,0:T(8,128)(2,1)S(1)}, u32[]{:S(2)}, u32[]{:S(2)}) collective-permute-start(bf16[384,512]{1,0:T(8,128)(2,1)S(1)} %constant_dynamic-slice_fusion), channel_id=1, source_target_pairs={{0,1},{1,0},{2,3},{3,2},{4,5},{5,4},{6,7},{7,6},{8,9},{9,8},{10,11... | collective-permute-start | bytes 1179656 | tf_op jit(solution)/shard_map/ppermute | solution.py:23
  223.2 5.2 %convolution_convert_fusion.1 = bf16[4,8192]{1,0:T(4,128)(2,1)} fusion(bf16[4,512]{1,0:T(4,128)(2,1)S(1)} %reduce_sum.24, bf16[512,8192]{1,0:T(8,128)(2,1)} %all-gather.2.cloned.1.call-done), kind=kOutput, calls=%fused_computation.1 | convolution fusion | flops 33587200 | bytes 8458240 | tf_op jit(solution)/shard_map/dot_general | solution.py:89
  228.4 4.0 %all-to-all-start.1 = ((bf16[16,4,512]{2,1,0:T(4,128)(2,1)}), bf16[16,4,512]{2,1,0:T(4,128)(2,1)S(1)}, u32[]{:S(2)}, u32[]{:S(2)}) async-start(bf16[16,4,512]{2,1,0:T(4,128)(2,1)} %bitcast.7), calls=%async_computation.2 | async-start | bytes 131072 | tf_op jit(solution)/shard_map/all_to_all | solution.py:93
  232.4 7.9 %all-to-all-done.1 = bf16[16,4,512]{2,1,0:T(4,128)(2,1)S(1)} async-done(((bf16[16,4,512]{2,1,0:T(4,128)(2,1)}), bf16[16,4,512]{2,1,0:T(4,128)(2,1)S(1)}, u32[]{:S(2)}, u32[]{:S(2)}) %all-to-all-start.1) | async-done | bytes 65568 | tf_op jit(solution)/shard_map/all_to_all | solution.py:93
  240.9 0.9 add_convert_fusion
  (29 shorter events, 4.0 us)
Async XLA Ops:
  7.2 125.8 %all-gather.2.cloned.1.call-start = ((), (), s32[]{:S(2)}) async-start(), calls=%async_computation.3 | async-start | bytes 8650752 | tf_op jit(solution)/shard_map/all_gather | solution.py:85
  7.9 211.0 %reduce-scatter.2.cloned.1.call-start = ((), (), s32[]{:S(2)}) async-start(), calls=%async_computation.4 | async-start | bytes 7077888 | tf_op jit(solution)/shard_map/reduce_scatter | solution.py:87
  8.7 59.9 %collective-permute-start = (bf16[3,2,512]{2,1,0:T(2,128)(2,1)S(1)}, bf16[3,2,512]{2,1,0:T(2,128)(2,1)S(1)}, u32[]{:S(2)}, u32[]{:S(2)}) collective-permute-start(bf16[3,2,512]{2,1,0:T(2,128)(2,1)S(1)} %slice.38), channel_id=1, source_target_pairs={{0,16},{16,32},{32,48},{48,64},{64,80},{80,96},{96,112},{112,128},... | collective-permute-start | bytes 18440 | tf_op jit(solution)/shard_map/ppermute | solution.py:15
  39.3 29.9 %copy-start = (bf16[3,384,512]{2,1,0:T(8,128)(2,1)S(1)}, bf16[3,384,512]{2,1,0:T(8,128)(2,1)}, u32[]{:S(2)}) copy-start(bf16[3,384,512]{2,1,0:T(8,128)(2,1)} %param.6) | copy-start | bytes 3538948
  68.6 0.6 copy-start.2
  70.9 5.7 %collective-permute-start.1 = (bf16[127,512]{1,0:T(8,128)(2,1)S(1)}, bf16[127,512]{1,0:T(8,128)(2,1)S(1)}, u32[]{:S(2)}, u32[]{:S(2)}) collective-permute-start(bf16[127,512]{1,0:T(8,128)(2,1)S(1)} %slice_bitcast_fusion.1), channel_id=1, source_target_pairs={{0,16},{16,32},{32,48},{48,64},{64,80},{80,96},{96,112},{112,128},... | collective-permute-start | bytes 390152 | tf_op jit(solution)/shard_map/ppermute | solution.py:15
  76.9 10.5 %copy-start.3 = (f32[512]{0:T(512)S(1)}, f32[512]{0:T(512)}, u32[]{:S(2)}) copy-start(f32[512]{0:T(512)} %param.9) | copy-start | bytes 6148
  85.9 1.8 copy-start.4
  219.9 21.0 %copy-start.1 = (bf16[384,1024]{1,0:T(8,128)(2,1)S(1)}, bf16[384,1024]{1,0:T(8,128)(2,1)}, u32[]{:S(2)}) copy-start(bf16[384,1024]{1,0:T(8,128)(2,1)} %reduce-scatter.2.cloned.1.call-done) | copy-start | bytes 2359300
  219.9 21.0 %collective-permute-start.2 = (bf16[384,512]{1,0:T(8,128)(2,1)S(1)}, bf16[384,512]{1,0:T(8,128)(2,1)S(1)}, u32[]{:S(2)}, u32[]{:S(2)}) collective-permute-start(bf16[384,512]{1,0:T(8,128)(2,1)S(1)} %constant_dynamic-slice_fusion), channel_id=1, source_target_pairs={{0,1},{1,0},{2,3},{3,2},{4,5},{5,4},{6,7},{7,6},{8,9},{9,8},{10,11... | collective-permute-start | bytes 1179656 | tf_op jit(solution)/shard_map/ppermute | solution.py:23
  228.4 11.9 %all-to-all-start.1 = ((bf16[16,4,512]{2,1,0:T(4,128)(2,1)}), bf16[16,4,512]{2,1,0:T(4,128)(2,1)S(1)}, u32[]{:S(2)}, u32[]{:S(2)}) async-start(bf16[16,4,512]{2,1,0:T(4,128)(2,1)} %bitcast.7), calls=%async_computation.2 | async-start | bytes 131072 | tf_op jit(solution)/shard_map/all_to_all | solution.py:93
Sparse Core Ops, SparseCore 0:
  11.1 121.7 all-gather.1
  141.8 77.0 reduce-scatter.1

commit v7 on v6

--- a/solution.py
+++ b/solution.py
@@ -83,13 +83,16 @@
     site_gated = exchange_scatter(picked_gated.astype(jnp.bfloat16), "context")
     gated, site_gated = lax.optimization_barrier((gated, site_gated))
     full_weight = lax.all_gather(out_weight, "context", axis=1, tiled=True)
-    terms = jnp.dot(gated, full_weight, preferred_element_type=jnp.float32)
-    partial = lax.psum_scatter(terms.astype(jnp.bfloat16), "z", scatter_dimension=1, tiled=True)
+    sites = site_gated.shape[0]
+    padding = jnp.zeros((-(rows + sites) % 8, width), gated.dtype)
+    both = jnp.concatenate([gated, site_gated, padding], axis=0)
+    both = jnp.dot(both, full_weight, preferred_element_type=jnp.float32).astype(jnp.bfloat16)
+    terms = both[:rows]
+    site_terms = both[rows : rows + sites]
+    partial = lax.psum_scatter(terms, "z", scatter_dimension=1, tiled=True)
     mixed = pair_scatter(partial, "x_lo")
-    site_terms = jnp.dot(site_gated, full_weight, preferred_element_type=jnp.float32)
-    site_terms = site_terms.astype(jnp.bfloat16)
     blocks = lax.axis_size(("z", "x_lo"))
-    site_terms = site_terms.reshape(site_terms.shape[0], blocks, width).transpose(1, 0, 2)
+    site_terms = site_terms.reshape(sites, blocks, width).transpose(1, 0, 2)
     site_terms = lax.all_to_all(site_terms, ("z", "x_lo"), 0, 0, tiled=True)
     variant_states = site_terms.astype(jnp.float32).sum(0).astype(jnp.bfloat16)
     return (mixed, variant_states)

time: 250 us -> 251 us (level)
  blocking collectives: 24.2 us -> 0 us
  starting transfers between devices: 14 us -> 26.6 us
  waiting for transfers between devices: 110 us -> 119 us
  local copies, waits for them, and re-layouts: 58.2 us -> 66.4 us
  matrix products: 23.2 us -> 16.7 us
    all_to_all x1 -> x0, blocking collectives: 24.2 us -> none  [exchange_scatter(): pieces = lax.all_to_all(pieces, axis, 0, 0, tiled=True)]
    all_to_all x0 -> x1, starting transfers between devices: none -> 12.8 us  [exchange_scatter(): pieces = lax.all_to_all(pieces, axis, 0, 0, tiled=True)]
    all_to_all x0 -> x1, waiting for transfers between devices: none -> 10.8 us  [exchange_scatter(): pieces = lax.all_to_all(pieces, axis, 0, 0, tiled=True)]
    dot_general x2 -> x1, matrix products: 13.9 us -> 7.41 us  [on_device(): jnp.dot(both, full_weight, preferred_element_type=jnp.float32)]
    slice x0 -> x2, local copies, waits for them, and re-layouts: none -> 4.65 us  [the longest x1 3.1 us: on_device(): terms = both[:rows]]
    unnamed x13, local copies, waits for them, and re-layouts: 13.2 us -> 15.9 us
  transfers between devices with their start and end apart: 6 -> 7, of which waited for: 4 -> 5; matrix products, arithmetic and copies ran while one was open for 30% -> 29% of each run, Pallas kernels for 0% -> 0%
where the time goes in v7:
time: 251 us; the launch traced here: 249 us
  waiting for transfers between devices  119 us (47%)
  local copies, waits for them, and re-layouts  66.4 us (26%)
  starting transfers between devices  26.6 us (11%)
  matrix products  16.7 us (7%)
  between operations  14.2 us (6%)
  other arithmetic  5.96 us (2%)
    reduce_scatter x1, waiting for transfers between devices, on_device(): partial = lax.psum_scatter(terms, 'z', scatter_dimension=1, tiled=True)  76.3 us
    reshape x1, local copies, waits for them, and re-layouts, banded_filters(): return tiled[:, :rows * span].reshape(local_groups, rows, span)  29.3 us
    all_gather x1, waiting for transfers between devices, on_device(): full_weight = lax.all_gather(out_weight, 'context', axis=1, tiled=True)  20.3 us
    unnamed x13, local copies, waits for them, and re-layouts  15.9 us
    all_to_all x1, starting transfers between devices, exchange_scatter(): pieces = lax.all_to_all(pieces, axis, 0, 0, tiled=True)  12.8 us
    all_to_all x1, waiting for transfers between devices, exchange_scatter(): pieces = lax.all_to_all(pieces, axis, 0, 0, tiled=True)  10.8 us
    dot_general x1, matrix products, on_device(): jnp.einsum('gim,mgc->igc', toeplitz, extended.reshape(span, local_groups,...  9.02 us
    all_to_all x1, waiting for transfers between devices, on_device(): site_terms = lax.all_to_all(site_terms, ('z', 'x_lo'), 0, 0, tiled=True)  7.89 us
  transfers between devices with their start and end apart: 7, of which 5 were waited for; matrix products, arithmetic and copies ran while one was open for 29% of the time, Pallas kernels for 0%

profile of v7, /device:TPU:1, one launch (start us, length us, event | category | flops | bytes accessed | tf_op | source)
XLA Modules:
  0.0 249.2 jit_solution(16767664909289436123)
XLA Ops:
  8.7 4.6 %collective-permute-start = (bf16[3,2,512]{2,1,0:T(2,128)(2,1)S(1)}, bf16[3,2,512]{2,1,0:T(2,128)(2,1)S(1)}, u32[]{:S(2)}, u32[]{:S(2)}) collective-permute-start(bf16[3,2,512]{2,1,0:T(2,128)(2,1)S(1)} %slice.44), channel_id=1, source_target_pairs={{0,16},{16,32},{32,48},{48,64},{64,80},{80,96},{96,112},{112,128},... | collective-permute-start | bytes 18440 | tf_op jit(solution)/shard_map/ppermute | solution.py:15
  14.1 1.2 broadcast_subtract_fusion
  16.7 5.4 %tile.4 = bf16[32,384,512]{2,1,0:T(8,128)(2,1)} broadcast(bf16[32,512]{1,0:T(8,128)(2,1)S(1)} %concatenate.14), dimensions={0,2} | broadcast | bytes 12615680 | tf_op jit(solution)/shard_map/tile | solution.py:51
  22.1 12.0 %copy.18 = bf16[4,8,384,512]{3,1,2,0:T(8,128)(2,1)S(1)} copy(bf16[4,8,384,512]{3,2,1,0:T(8,128)(2,1)} %bitcast.31) | data formatting | bytes 25165824
  34.2 5.2 %slice.62 = bf16[32,196224]{1,0:T(8,128)(2,1)} slice(bf16[32,196608]{1,0:T(8,128)(2,1)S(1)} %bitcast.32), slice={[0:32], [0:196224]} | slice | bytes 25116672 | tf_op jit(solution)/shard_map/slice | solution.py:52
  39.3 29.3 %reshape.29 = bf16[32,384,511]{2,1,0:T(8,128)(2,1)} reshape(bf16[32,196224]{1,0:T(8,128)(2,1)} %slice.62) | data formatting | bytes 25116672 | tf_op jit(solution)/shard_map/reshape | solution.py:52
  69.3 1.5 multiply_add_fusion
  71.0 2.1 collective-permute-start.1
  73.2 3.4 %collective-permute-done.1 = bf16[127,512]{1,0:T(8,128)(2,1)S(1)} collective-permute-done((bf16[127,512]{1,0:T(8,128)(2,1)S(1)}, bf16[127,512]{1,0:T(8,128)(2,1)S(1)}, u32[]{:S(2)}, u32[]{:S(2)}) %collective-permute-start.1) | collective-permute-done | bytes 130080 | tf_op jit(solution)/shard_map/ppermute | solution.py:15
  76.9 9.0 %fusion.12 = f32[32,16,384]{2,1,0:T(8,128)} fusion(bf16[511,32,16]{0,2,1:T(8,128)(2,1)S(1)} %bitcast.34, bf16[32,384,511]{2,1,0:T(8,128)(2,1)} %reshape.29), kind=kOutput, calls=%fused_computation.29 | convolution fusion | flops 200933376 | bytes 13868032 | tf_op jit(solution)/shard_map/gim,mgc->igc/dot_general | solution.py:69
  86.0 1.4 copy.13
  88.8 12.8 %all-to-all-start = ((bf16[32,4,512]{2,1,0:T(4,128)(2,1)}), bf16[32,4,512]{2,1,0:T(4,128)(2,1)S(1)}, u32[]{:S(2)}, u32[]{:S(2)}) async-start(bf16[32,4,512]{2,1,0:T(4,128)(2,1)} %reshape.31), calls=%async_computation | async-start | bytes 262144 | tf_op jit(solution)/shard_map/all_to_all | solution.py:30
  101.7 10.8 %all-to-all-done = bf16[32,4,512]{2,1,0:T(4,128)(2,1)S(1)} async-done(((bf16[32,4,512]{2,1,0:T(4,128)(2,1)}), bf16[32,4,512]{2,1,0:T(4,128)(2,1)S(1)}, u32[]{:S(2)}, u32[]{:S(2)}) %all-to-all-start) | async-done | bytes 131104 | tf_op jit(solution)/shard_map/all_to_all | solution.py:30
  112.5 20.3 %all-gather.2.cloned.1.call-done = bf16[512,8192]{1,0:T(8,128)(2,1)} async-done(((bf16[512,256]{1,0:T(8,128)(2,1)}), bf16[512,8192]{1,0:T(8,128)(2,1)}) %all-gather.2.cloned.1.call-update) | async-done | bytes 8388624 | tf_op jit(solution)/shard_map/all_gather | solution.py:85
  132.8 7.4 %convolution_convert_fusion = bf16[392,8192]{1,0:T(8,128)(2,1)S(1)} fusion(bf16[512,8192]{1,0:T(8,128)(2,1)} %all-gather.2.cloned.1.call-done, bf16[4,512]{1,0:T(4,128)(2,1)S(1)} %reduce_sum.24, bf16[384,512]{1,0:T(8,128)(2,1)S(1)} %fusion.3, bf16[392]{0:T(512)(128)(2,1)S(1)} %pad.3.clone), kind=kOutput, calls=%fused_computation | convolution fusion | flops 3292749824 | bytes 15209232 | tf_op jit(solution)/shard_map/dot_general | solution.py:89
  140.2 2.7 %copy-done = bf16[392,8192]{1,0:T(8,128)(2,1)} copy-done((bf16[392,8192]{1,0:T(8,128)(2,1)}, bf16[392,8192]{1,0:T(8,128)(2,1)S(1)}, u32[]{:S(2)}) %copy-start) | copy-done | bytes 6422552
  142.9 3.1 %slice.63 = bf16[384,8192]{1,0:T(8,128)(2,1)} slice(bf16[392,8192]{1,0:T(8,128)(2,1)S(1)} %convolution_convert_fusion), slice={[0:384], [0:8192]} | slice | bytes 12582912 | tf_op jit(solution)/shard_map/slice | solution.py:90
  146.1 76.3 %reduce-scatter.2.cloned.1.call-done = bf16[384,1024]{1,0:T(8,128)(2,1)} async-done(((bf16[384,8192]{1,0:T(8,128)(2,1)}), bf16[384,1024]{1,0:T(8,128)(2,1)}) %reduce-scatter.2.cloned.1.call-update) | async-done | bytes 786448 | tf_op jit(solution)/shard_map/reduce_scatter | solution.py:92
  222.3 1.0 constant_dynamic-slice_fusion
  223.4 3.1 %collective-permute-start.2 = (bf16[384,512]{1,0:T(8,128)(2,1)S(1)}, bf16[384,512]{1,0:T(8,128)(2,1)S(1)}, u32[]{:S(2)}, u32[]{:S(2)}) collective-permute-start(bf16[384,512]{1,0:T(8,128)(2,1)S(1)} %constant_dynamic-slice_fusion), channel_id=1, source_target_pairs={{0,1},{1,0},{2,3},{3,2},{4,5},{5,4},{6,7},{7,6},{8,9},{9,8},{10,11... | collective-permute-start | bytes 1179656 | tf_op jit(solution)/shard_map/ppermute | solution.py:23
  226.5 1.6 slice.64
  228.0 4.0 %all-to-all-start.1 = ((bf16[16,4,512]{2,1,0:T(4,128)(2,1)}), bf16[16,4,512]{2,1,0:T(4,128)(2,1)S(1)}, u32[]{:S(2)}, u32[]{:S(2)}) async-start(bf16[16,4,512]{2,1,0:T(4,128)(2,1)} %bitcast.7), calls=%async_computation.2 | async-start | bytes 131072 | tf_op jit(solution)/shard_map/all_to_all | solution.py:96
  232.0 7.9 %all-to-all-done.1 = bf16[16,4,512]{2,1,0:T(4,128)(2,1)S(1)} async-done(((bf16[16,4,512]{2,1,0:T(4,128)(2,1)}), bf16[16,4,512]{2,1,0:T(4,128)(2,1)S(1)}, u32[]{:S(2)}, u32[]{:S(2)}) %all-to-all-start.1) | async-done | bytes 65568 | tf_op jit(solution)/shard_map/all_to_all | solution.py:96
  240.6 1.8 add_convert_fusion
  (33 shorter events, 7.1 us)
Async XLA Ops:
  7.2 125.6 %all-gather.2.cloned.1.call-start = ((), (), s32[]{:S(2)}) async-start(), calls=%async_computation.3 | async-start | bytes 8650752 | tf_op jit(solution)/shard_map/all_gather | solution.py:85
  8.7 60.0 %collective-permute-start = (bf16[3,2,512]{2,1,0:T(2,128)(2,1)S(1)}, bf16[3,2,512]{2,1,0:T(2,128)(2,1)S(1)}, u32[]{:S(2)}, u32[]{:S(2)}) collective-permute-start(bf16[3,2,512]{2,1,0:T(2,128)(2,1)S(1)} %slice.44), channel_id=1, source_target_pairs={{0,16},{16,32},{32,48},{48,64},{64,80},{80,96},{96,112},{112,128},... | collective-permute-start | bytes 18440 | tf_op jit(solution)/shard_map/ppermute | solution.py:15
  39.3 29.9 %copy-start.1 = (bf16[3,384,512]{2,1,0:T(8,128)(2,1)S(1)}, bf16[3,384,512]{2,1,0:T(8,128)(2,1)}, u32[]{:S(2)}) copy-start(bf16[3,384,512]{2,1,0:T(8,128)(2,1)} %param.6) | copy-start | bytes 3538948
  68.7 0.6 copy-start.2
  71.0 5.7 %collective-permute-start.1 = (bf16[127,512]{1,0:T(8,128)(2,1)S(1)}, bf16[127,512]{1,0:T(8,128)(2,1)S(1)}, u32[]{:S(2)}, u32[]{:S(2)}) collective-permute-start(bf16[127,512]{1,0:T(8,128)(2,1)S(1)} %slice_bitcast_fusion.1), channel_id=1, source_target_pairs={{0,16},{16,32},{32,48},{48,64},{64,80},{80,96},{96,112},{112,128},... | collective-permute-start | bytes 390152 | tf_op jit(solution)/shard_map/ppermute | solution.py:15
  76.9 10.4 %copy-start.3 = (f32[512]{0:T(512)S(1)}, f32[512]{0:T(512)}, u32[]{:S(2)}) copy-start(f32[512]{0:T(512)} %param.9) | copy-start | bytes 6148
  86.0 1.8 copy-start.4
  88.8 23.7 %all-to-all-start = ((bf16[32,4,512]{2,1,0:T(4,128)(2,1)}), bf16[32,4,512]{2,1,0:T(4,128)(2,1)S(1)}, u32[]{:S(2)}, u32[]{:S(2)}) async-start(bf16[32,4,512]{2,1,0:T(4,128)(2,1)} %reshape.31), calls=%async_computation | async-start | bytes 262144 | tf_op jit(solution)/shard_map/all_to_all | solution.py:30
  101.5 120.8 %reduce-scatter.2.cloned.1.call-start = ((), (), s32[]{:S(2)}) async-start(), calls=%async_computation.4 | async-start | bytes 7077888 | tf_op jit(solution)/shard_map/reduce_scatter | solution.py:92
  140.2 2.7 %copy-start = (bf16[392,8192]{1,0:T(8,128)(2,1)}, bf16[392,8192]{1,0:T(8,128)(2,1)S(1)}, u32[]{:S(2)}) copy-start(bf16[392,8192]{1,0:T(8,128)(2,1)S(1)} %convolution_convert_fusion) | copy-start | bytes 19267588
  223.4 17.2 %collective-permute-start.2 = (bf16[384,512]{1,0:T(8,128)(2,1)S(1)}, bf16[384,512]{1,0:T(8,128)(2,1)S(1)}, u32[]{:S(2)}, u32[]{:S(2)}) collective-permute-start(bf16[384,512]{1,0:T(8,128)(2,1)S(1)} %constant_dynamic-slice_fusion), channel_id=1, source_target_pairs={{0,1},{1,0},{2,3},{3,2},{4,5},{5,4},{6,7},{7,6},{8,9},{9,8},{10,11... | collective-permute-start | bytes 1179656 | tf_op jit(solution)/shard_map/ppermute | solution.py:23
  228.0 11.9 %all-to-all-start.1 = ((bf16[16,4,512]{2,1,0:T(4,128)(2,1)}), bf16[16,4,512]{2,1,0:T(4,128)(2,1)S(1)}, u32[]{:S(2)}, u32[]{:S(2)}) async-start(bf16[16,4,512]{2,1,0:T(4,128)(2,1)} %bitcast.7), calls=%async_computation.2 | async-start | bytes 131072 | tf_op jit(solution)/shard_map/all_to_all | solution.py:96
Sparse Core Ops, SparseCore 0:
  11.1 121.6 all-gather.1
  146.2 76.1 reduce-scatter.1

commit v8 on v7

--- a/solution.py
+++ b/solution.py
@@ -87,14 +87,10 @@
     padding = jnp.zeros((-(rows + sites) % 8, width), gated.dtype)
     both = jnp.concatenate([gated, site_gated, padding], axis=0)
     both = jnp.dot(both, full_weight, preferred_element_type=jnp.float32).astype(jnp.bfloat16)
-    terms = both[:rows]
-    site_terms = both[rows : rows + sites]
-    partial = lax.psum_scatter(terms, "z", scatter_dimension=1, tiled=True)
-    mixed = pair_scatter(partial, "x_lo")
-    blocks = lax.axis_size(("z", "x_lo"))
-    site_terms = site_terms.reshape(sites, blocks, width).transpose(1, 0, 2)
-    site_terms = lax.all_to_all(site_terms, ("z", "x_lo"), 0, 0, tiled=True)
-    variant_states = site_terms.astype(jnp.float32).sum(0).astype(jnp.bfloat16)
+    partial = lax.psum_scatter(both, "z", scatter_dimension=1, tiled=True)
+    reduced = pair_scatter(partial, "x_lo")
+    mixed = reduced[:rows]
+    variant_states = reduced[rows : rows + sites]
     return (mixed, variant_states)
 
 

time: 251 us -> 243 us (0.968)
  local copies, waits for them, and re-layouts: 66.4 us -> 60.4 us
  starting transfers between devices: 26.6 us -> 22.6 us
  waiting for transfers between devices: 119 us -> 122 us
    ppermute x1, waiting for transfers between devices: 0.01 us -> 9.01 us  [pair_scatter(): got = lax.ppermute(send, axis, [(0, 1), (1, 0)])]
    all_to_all x1 -> x0, waiting for transfers between devices: 7.89 us -> none  [on_device(): site_terms = lax.all_to_all(site_terms, ('z', 'x_lo'), 0, 0, tiled=True)]
    all_to_all x1 -> x0, starting transfers between devices: 3.99 us -> none  [on_device(): site_terms = lax.all_to_all(site_terms, ('z', 'x_lo'), 0, 0, tiled=True)]
    slice x2, local copies, waits for them, and re-layouts: 4.65 us -> 1.37 us  [the longest x1 0.77 us: on_device(): mixed = reduced[:rows]]
    unnamed x13 -> x11, local copies, waits for them, and re-layouts: 15.9 us -> 13.2 us
  transfers between devices with their start and end apart: 7 -> 6, of which waited for: 5 -> 5; matrix products, arithmetic and copies ran while one was open for 29% -> 29% of each run, Pallas kernels for 0% -> 0%
where the time goes in v8:
time: 243 us; the launch traced here: 242 us
  waiting for transfers between devices  122 us (50%)
  local copies, waits for them, and re-layouts  60.4 us (25%)
  starting transfers between devices  22.6 us (9%)
  matrix products  18.4 us (8%)
  between operations  14.2 us (6%)
  other arithmetic  4.59 us (2%)
    reduce_scatter x1, waiting for transfers between devices, on_device(): partial = lax.psum_scatter(both, 'z', scatter_dimension=1, tiled=True)  77.5 us
    reshape x1, local copies, waits for them, and re-layouts, banded_filters(): return tiled[:, :rows * span].reshape(local_groups, rows, span)  29.3 us
    all_gather x1, waiting for transfers between devices, on_device(): full_weight = lax.all_gather(out_weight, 'context', axis=1, tiled=True)  20.3 us
    unnamed x11, local copies, waits for them, and re-layouts  13.2 us
    all_to_all x1, starting transfers between devices, exchange_scatter(): pieces = lax.all_to_all(pieces, axis, 0, 0, tiled=True)  12.8 us
    all_to_all x1, waiting for transfers between devices, exchange_scatter(): pieces = lax.all_to_all(pieces, axis, 0, 0, tiled=True)  10.8 us
    dot_general x1, matrix products, on_device(): jnp.dot(both, full_weight, preferred_element_type=jnp.float32)  9.14 us
    dot_general x1, matrix products, on_device(): jnp.einsum('gim,mgc->igc', toeplitz, extended.reshape(span, local_groups,...  9.02 us
  transfers between devices with their start and end apart: 6, of which 5 were waited for; matrix products, arithmetic and copies ran while one was open for 29% of the time, Pallas kernels for 0%

profile of v8, /device:TPU:1, one launch (start us, length us, event | category | flops | bytes accessed | tf_op | source)
XLA Modules:
  0.0 241.9 jit_solution(587590781040510108)
XLA Ops:
  7.9 0.8 slice.44
  8.7 4.6 %collective-permute-start = (bf16[3,2,512]{2,1,0:T(2,128)(2,1)S(1)}, bf16[3,2,512]{2,1,0:T(2,128)(2,1)S(1)}, u32[]{:S(2)}, u32[]{:S(2)}) collective-permute-start(bf16[3,2,512]{2,1,0:T(2,128)(2,1)S(1)} %slice.44), channel_id=1, source_target_pairs={{0,16},{16,32},{32,48},{48,64},{64,80},{80,96},{96,112},{112,128},... | collective-permute-start | bytes 18440 | tf_op jit(solution)/shard_map/ppermute | solution.py:15
  13.3 0.9 fusion.11
  14.1 1.2 broadcast_subtract_fusion
  15.9 0.8 rev.4
  16.7 5.4 %tile.4 = bf16[32,384,512]{2,1,0:T(8,128)(2,1)} broadcast(bf16[32,512]{1,0:T(8,128)(2,1)S(1)} %concatenate.14), dimensions={0,2} | broadcast | bytes 12615680 | tf_op jit(solution)/shard_map/tile | solution.py:51
  22.1 12.0 %copy.15 = bf16[4,8,384,512]{3,1,2,0:T(8,128)(2,1)S(1)} copy(bf16[4,8,384,512]{3,2,1,0:T(8,128)(2,1)} %bitcast.28) | data formatting | bytes 25165824
  34.2 5.2 %slice.62 = bf16[32,196224]{1,0:T(8,128)(2,1)} slice(bf16[32,196608]{1,0:T(8,128)(2,1)S(1)} %bitcast.29), slice={[0:32], [0:196224]} | slice | bytes 25116672 | tf_op jit(solution)/shard_map/slice | solution.py:52
  39.3 29.3 %reshape.26 = bf16[32,384,511]{2,1,0:T(8,128)(2,1)} reshape(bf16[32,196224]{1,0:T(8,128)(2,1)} %slice.62) | data formatting | bytes 25116672 | tf_op jit(solution)/shard_map/reshape | solution.py:52
  69.3 1.5 multiply_add_fusion
  71.0 2.1 collective-permute-start.1
  73.2 3.4 %collective-permute-done.1 = bf16[127,512]{1,0:T(8,128)(2,1)S(1)} collective-permute-done((bf16[127,512]{1,0:T(8,128)(2,1)S(1)}, bf16[127,512]{1,0:T(8,128)(2,1)S(1)}, u32[]{:S(2)}, u32[]{:S(2)}) %collective-permute-start.1) | collective-permute-done | bytes 130080 | tf_op jit(solution)/shard_map/ppermute | solution.py:15
  76.9 9.0 %fusion.12 = f32[32,16,384]{2,1,0:T(8,128)} fusion(bf16[511,32,16]{0,2,1:T(8,128)(2,1)S(1)} %bitcast.31, bf16[32,384,511]{2,1,0:T(8,128)(2,1)} %reshape.26), kind=kOutput, calls=%fused_computation.29 | convolution fusion | flops 200933376 | bytes 13868032 | tf_op jit(solution)/shard_map/gim,mgc->igc/dot_general | solution.py:69
  86.0 1.4 copy.11
  88.8 12.8 %all-to-all-start = ((bf16[32,4,512]{2,1,0:T(4,128)(2,1)}), bf16[32,4,512]{2,1,0:T(4,128)(2,1)S(1)}, u32[]{:S(2)}, u32[]{:S(2)}) async-start(bf16[32,4,512]{2,1,0:T(4,128)(2,1)} %reshape.28), calls=%async_computation | async-start | bytes 262144 | tf_op jit(solution)/shard_map/all_to_all | solution.py:30
  101.7 10.8 %all-to-all-done = bf16[32,4,512]{2,1,0:T(4,128)(2,1)S(1)} async-done(((bf16[32,4,512]{2,1,0:T(4,128)(2,1)}), bf16[32,4,512]{2,1,0:T(4,128)(2,1)S(1)}, u32[]{:S(2)}, u32[]{:S(2)}) %all-to-all-start) | async-done | bytes 131104 | tf_op jit(solution)/shard_map/all_to_all | solution.py:30
  112.5 20.3 %all-gather.2.cloned.1.call-done = bf16[512,8192]{1,0:T(8,128)(2,1)} async-done(((bf16[512,256]{1,0:T(8,128)(2,1)}), bf16[512,8192]{1,0:T(8,128)(2,1)}) %all-gather.2.cloned.1.call-update) | async-done | bytes 8388624 | tf_op jit(solution)/shard_map/all_gather | solution.py:85
  132.8 9.1 %convolution_convert_fusion = bf16[392,8192]{1,0:T(8,128)(2,1)} fusion(bf16[512,8192]{1,0:T(8,128)(2,1)} %all-gather.2.cloned.1.call-done, bf16[4,512]{1,0:T(4,128)(2,1)S(1)} %reduce_sum.12, bf16[384,512]{1,0:T(8,128)(2,1)S(1)} %fusion.3, bf16[392]{0:T(512)(128)(2,1)S(1)} %pad.3.clone), kind=kOutput, calls=%fused_computation | convolution fusion | flops 3292749824 | bytes 15209232 | tf_op jit(solution)/shard_map/dot_general | solution.py:89
  142.0 77.5 %reduce-scatter.2.cloned.1.call-done = bf16[392,1024]{1,0:T(8,128)(2,1)} async-done(((bf16[392,8192]{1,0:T(8,128)(2,1)}), bf16[392,1024]{1,0:T(8,128)(2,1)}) %reduce-scatter.2.cloned.1.call-update) | async-done | bytes 802832 | tf_op jit(solution)/shard_map/reduce_scatter | solution.py:90
  219.5 1.0 constant_dynamic-slice_fusion
  220.5 3.1 %collective-permute-start.2 = (bf16[392,512]{1,0:T(8,128)(2,1)S(1)}, bf16[392,512]{1,0:T(8,128)(2,1)S(1)}, u32[]{:S(2)}, u32[]{:S(2)}) collective-permute-start(bf16[392,512]{1,0:T(8,128)(2,1)S(1)} %constant_dynamic-slice_fusion), channel_id=1, source_target_pairs={{0,1},{1,0},{2,3},{3,2},{4,5},{5,4},{6,7},{7,6},{8,9},{9,8},{10,11... | collective-permute-start | bytes 1204232 | tf_op jit(solution)/shard_map/ppermute | solution.py:23
  223.6 9.0 %collective-permute-done.2 = bf16[392,512]{1,0:T(8,128)(2,1)S(1)} collective-permute-done((bf16[392,512]{1,0:T(8,128)(2,1)S(1)}, bf16[392,512]{1,0:T(8,128)(2,1)S(1)}, u32[]{:S(2)}, u32[]{:S(2)}) %collective-permute-start.2) | collective-permute-done | bytes 401440 | tf_op jit(solution)/shard_map/ppermute | solution.py:23
  232.6 1.1 add_convert_fusion
  233.7 0.8 slice.63
  (28 shorter events, 4.7 us)
Async XLA Ops:
  7.2 125.6 %all-gather.2.cloned.1.call-start = ((), (), s32[]{:S(2)}) async-start(), calls=%async_computation.2 | async-start | bytes 8650752 | tf_op jit(solution)/shard_map/all_gather | solution.py:85
  8.7 60.0 %collective-permute-start = (bf16[3,2,512]{2,1,0:T(2,128)(2,1)S(1)}, bf16[3,2,512]{2,1,0:T(2,128)(2,1)S(1)}, u32[]{:S(2)}, u32[]{:S(2)}) collective-permute-start(bf16[3,2,512]{2,1,0:T(2,128)(2,1)S(1)} %slice.44), channel_id=1, source_target_pairs={{0,16},{16,32},{32,48},{48,64},{64,80},{80,96},{96,112},{112,128},... | collective-permute-start | bytes 18440 | tf_op jit(solution)/shard_map/ppermute | solution.py:15
  39.3 29.9 %copy-start = (bf16[3,384,512]{2,1,0:T(8,128)(2,1)S(1)}, bf16[3,384,512]{2,1,0:T(8,128)(2,1)}, u32[]{:S(2)}) copy-start(bf16[3,384,512]{2,1,0:T(8,128)(2,1)} %param.6) | copy-start | bytes 3538948
  68.7 0.6 copy-start.1
  71.0 5.7 %collective-permute-start.1 = (bf16[127,512]{1,0:T(8,128)(2,1)S(1)}, bf16[127,512]{1,0:T(8,128)(2,1)S(1)}, u32[]{:S(2)}, u32[]{:S(2)}) collective-permute-start(bf16[127,512]{1,0:T(8,128)(2,1)S(1)} %slice_bitcast_fusion.1), channel_id=1, source_target_pairs={{0,16},{16,32},{32,48},{48,64},{64,80},{80,96},{96,112},{112,128},... | collective-permute-start | bytes 390152 | tf_op jit(solution)/shard_map/ppermute | solution.py:15
  76.9 10.4 %copy-start.2 = (f32[512]{0:T(512)S(1)}, f32[512]{0:T(512)}, u32[]{:S(2)}) copy-start(f32[512]{0:T(512)} %param.9) | copy-start | bytes 6148
  86.0 1.8 copy-start.3
  88.8 23.7 %all-to-all-start = ((bf16[32,4,512]{2,1,0:T(4,128)(2,1)}), bf16[32,4,512]{2,1,0:T(4,128)(2,1)S(1)}, u32[]{:S(2)}, u32[]{:S(2)}) async-start(bf16[32,4,512]{2,1,0:T(4,128)(2,1)} %reshape.28), calls=%async_computation | async-start | bytes 262144 | tf_op jit(solution)/shard_map/all_to_all | solution.py:30
  101.5 118.0 %reduce-scatter.2.cloned.1.call-start = ((), (), s32[]{:S(2)}) async-start(), calls=%async_computation.3 | async-start | bytes 7225344 | tf_op jit(solution)/shard_map/reduce_scatter | solution.py:90
  220.5 12.1 %collective-permute-start.2 = (bf16[392,512]{1,0:T(8,128)(2,1)S(1)}, bf16[392,512]{1,0:T(8,128)(2,1)S(1)}, u32[]{:S(2)}, u32[]{:S(2)}) collective-permute-start(bf16[392,512]{1,0:T(8,128)(2,1)S(1)} %constant_dynamic-slice_fusion), channel_id=1, source_target_pairs={{0,1},{1,0},{2,3},{3,2},{4,5},{5,4},{6,7},{7,6},{8,9},{9,8},{10,11... | collective-permute-start | bytes 1204232 | tf_op jit(solution)/shard_map/ppermute | solution.py:23
Sparse Core Ops, SparseCore 0:
  11.1 121.6 all-gather.1
  142.1 77.3 reduce-scatter.1

commit v9 on v8

--- a/solution.py
+++ b/solution.py
@@ -85,7 +85,7 @@
     full_weight = lax.all_gather(out_weight, "context", axis=1, tiled=True)
     sites = site_gated.shape[0]
     padding = jnp.zeros((-(rows + sites) % 8, width), gated.dtype)
-    both = jnp.concatenate([gated, site_gated, padding], axis=0)
+    both = lax.optimization_barrier(jnp.concatenate([gated, site_gated, padding], axis=0))
     both = jnp.dot(both, full_weight, preferred_element_type=jnp.float32).astype(jnp.bfloat16)
     partial = lax.psum_scatter(both, "z", scatter_dimension=1, tiled=True)
     reduced = pair_scatter(partial, "x_lo")

time: 243 us -> 242 us (level)
  no operation moved by 1% of the time
where the time goes in v9:
time: 242 us
  waiting for transfers between devices  122 us (50%)
  local copies, waits for them, and re-layouts  60.4 us (25%)
  starting transfers between devices  22.6 us (9%)
  matrix products  18.2 us (8%)
  between operations  14.2 us (6%)
  other arithmetic  4.73 us (2%)
    reduce_scatter x1, waiting for transfers between devices, on_device(): partial = lax.psum_scatter(both, 'z', scatter_dimension=1, tiled=True)  77.5 us
    reshape x1, local copies, waits for them, and re-layouts, banded_filters(): return tiled[:, :rows * span].reshape(local_groups, rows, span)  29.3 us
    all_gather x1, waiting for transfers between devices, on_device(): full_weight = lax.all_gather(out_weight, 'context', axis=1, tiled=True)  20.2 us
    unnamed x11, local copies, waits for them, and re-layouts  13.2 us
    all_to_all x1, starting transfers between devices, exchange_scatter(): pieces = lax.all_to_all(pieces, axis, 0, 0, tiled=True)  12.8 us
    all_to_all x1, waiting for transfers between devices, exchange_scatter(): pieces = lax.all_to_all(pieces, axis, 0, 0, tiled=True)  10.8 us
    dot_general x1, matrix products, on_device(): jnp.einsum('gim,mgc->igc', toeplitz, extended.reshape(span, local_groups,...  9.02 us
    ppermute x1, waiting for transfers between devices, pair_scatter(): got = lax.ppermute(send, axis, [(0, 1), (1, 0)])  9 us
  transfers between devices with their start and end apart: 6, of which 5 were waited for; matrix products, arithmetic and copies ran while one was open for 29% of the time, Pallas kernels for 0%

profile of v9, /device:TPU:1, one launch (start us, length us, event | category | flops | bytes accessed | tf_op | source)
XLA Modules:
  0.0 241.7 jit_solution(7688944672993362209)
XLA Ops:
  7.9 0.8 slice.44
  8.7 4.6 %collective-permute-start = (bf16[3,2,512]{2,1,0:T(2,128)(2,1)S(1)}, bf16[3,2,512]{2,1,0:T(2,128)(2,1)S(1)}, u32[]{:S(2)}, u32[]{:S(2)}) collective-permute-start(bf16[3,2,512]{2,1,0:T(2,128)(2,1)S(1)} %slice.44), channel_id=1, source_target_pairs={{0,16},{16,32},{32,48},{48,64},{64,80},{80,96},{96,112},{112,128},... | collective-permute-start | bytes 18440 | tf_op jit(solution)/shard_map/ppermute | solution.py:15
  13.3 0.9 fusion.5
  14.1 1.2 broadcast_subtract_fusion
  15.9 0.8 rev.4
  16.7 5.4 %tile.4 = bf16[32,384,512]{2,1,0:T(8,128)(2,1)} broadcast(bf16[32,512]{1,0:T(8,128)(2,1)S(1)} %concatenate.14), dimensions={0,2} | broadcast | bytes 12615680 | tf_op jit(solution)/shard_map/tile | solution.py:51
  22.1 12.0 %copy.15 = bf16[4,8,384,512]{3,1,2,0:T(8,128)(2,1)S(1)} copy(bf16[4,8,384,512]{3,2,1,0:T(8,128)(2,1)} %bitcast.29) | data formatting | bytes 25165824
  34.2 5.2 %slice.62 = bf16[32,196224]{1,0:T(8,128)(2,1)} slice(bf16[32,196608]{1,0:T(8,128)(2,1)S(1)} %bitcast.30), slice={[0:32], [0:196224]} | slice | bytes 25116672 | tf_op jit(solution)/shard_map/slice | solution.py:52
  39.3 29.3 %reshape.26 = bf16[32,384,511]{2,1,0:T(8,128)(2,1)} reshape(bf16[32,196224]{1,0:T(8,128)(2,1)} %slice.62) | data formatting | bytes 25116672 | tf_op jit(solution)/shard_map/reshape | solution.py:52
  69.3 1.5 multiply_add_fusion
  71.0 2.1 collective-permute-start.1
  73.2 3.4 %collective-permute-done.1 = bf16[127,512]{1,0:T(8,128)(2,1)S(1)} collective-permute-done((bf16[127,512]{1,0:T(8,128)(2,1)S(1)}, bf16[127,512]{1,0:T(8,128)(2,1)S(1)}, u32[]{:S(2)}, u32[]{:S(2)}) %collective-permute-start.1) | collective-permute-done | bytes 130080 | tf_op jit(solution)/shard_map/ppermute | solution.py:15
  76.9 9.0 %fusion.6 = f32[32,16,384]{2,1,0:T(8,128)} fusion(bf16[511,32,16]{0,2,1:T(8,128)(2,1)S(1)} %bitcast.32, bf16[32,384,511]{2,1,0:T(8,128)(2,1)} %reshape.26), kind=kOutput, calls=%fused_computation.24 | convolution fusion | flops 200933376 | bytes 13868032 | tf_op jit(solution)/shard_map/gim,mgc->igc/dot_general | solution.py:69
  86.0 1.4 copy.11
  88.8 12.8 %all-to-all-start = ((bf16[32,4,512]{2,1,0:T(4,128)(2,1)}), bf16[32,4,512]{2,1,0:T(4,128)(2,1)S(1)}, u32[]{:S(2)}, u32[]{:S(2)}) async-start(bf16[32,4,512]{2,1,0:T(4,128)(2,1)} %reshape.28), calls=%async_computation | async-start | bytes 262144 | tf_op jit(solution)/shard_map/all_to_all | solution.py:30
  101.7 10.8 %all-to-all-done = bf16[32,4,512]{2,1,0:T(4,128)(2,1)S(1)} async-done(((bf16[32,4,512]{2,1,0:T(4,128)(2,1)}), bf16[32,4,512]{2,1,0:T(4,128)(2,1)S(1)}, u32[]{:S(2)}, u32[]{:S(2)}) %all-to-all-start) | async-done | bytes 131104 | tf_op jit(solution)/shard_map/all_to_all | solution.py:30
  112.6 20.2 %all-gather.2.cloned.1.call-done = bf16[512,8192]{1,0:T(8,128)(2,1)} async-done(((bf16[512,256]{1,0:T(8,128)(2,1)}), bf16[512,8192]{1,0:T(8,128)(2,1)}) %all-gather.2.cloned.1.call-update) | async-done | bytes 8388624 | tf_op jit(solution)/shard_map/all_gather | solution.py:85
  132.8 8.9 %convolution_convert_fusion = bf16[392,8192]{1,0:T(8,128)(2,1)} fusion(bf16[392,512]{1,0:T(8,128)(2,1)S(1)} %maximum_maximum_fusion, bf16[512,8192]{1,0:T(8,128)(2,1)} %all-gather.2.cloned.1.call-done), kind=kOutput, calls=%fused_computation | convolution fusion | flops 3291545600 | bytes 15212544 | tf_op jit(solution)/shard_map/dot_general | solution.py:89
  141.7 77.5 %reduce-scatter.2.cloned.1.call-done = bf16[392,1024]{1,0:T(8,128)(2,1)} async-done(((bf16[392,8192]{1,0:T(8,128)(2,1)}), bf16[392,1024]{1,0:T(8,128)(2,1)}) %reduce-scatter.2.cloned.1.call-update) | async-done | bytes 802832 | tf_op jit(solution)/shard_map/reduce_scatter | solution.py:90
  219.2 1.0 constant_dynamic-slice_fusion
  220.3 3.1 %collective-permute-start.2 = (bf16[392,512]{1,0:T(8,128)(2,1)S(1)}, bf16[392,512]{1,0:T(8,128)(2,1)S(1)}, u32[]{:S(2)}, u32[]{:S(2)}) collective-permute-start(bf16[392,512]{1,0:T(8,128)(2,1)S(1)} %constant_dynamic-slice_fusion), channel_id=1, source_target_pairs={{0,1},{1,0},{2,3},{3,2},{4,5},{5,4},{6,7},{7,6},{8,9},{9,8},{10,11... | collective-permute-start | bytes 1204232 | tf_op jit(solution)/shard_map/ppermute | solution.py:23
  223.4 9.0 %collective-permute-done.2 = bf16[392,512]{1,0:T(8,128)(2,1)S(1)} collective-permute-done((bf16[392,512]{1,0:T(8,128)(2,1)S(1)}, bf16[392,512]{1,0:T(8,128)(2,1)S(1)}, u32[]{:S(2)}, u32[]{:S(2)}) %collective-permute-start.2) | collective-permute-done | bytes 401440 | tf_op jit(solution)/shard_map/ppermute | solution.py:23
  232.4 1.1 add_convert_fusion
  233.5 0.8 slice.63
  (29 shorter events, 4.8 us)
Async XLA Ops:
  7.2 125.6 %all-gather.2.cloned.1.call-start = ((), (), s32[]{:S(2)}) async-start(), calls=%async_computation.2 | async-start | bytes 8650752 | tf_op jit(solution)/shard_map/all_gather | solution.py:85
  8.7 60.0 %collective-permute-start = (bf16[3,2,512]{2,1,0:T(2,128)(2,1)S(1)}, bf16[3,2,512]{2,1,0:T(2,128)(2,1)S(1)}, u32[]{:S(2)}, u32[]{:S(2)}) collective-permute-start(bf16[3,2,512]{2,1,0:T(2,128)(2,1)S(1)} %slice.44), channel_id=1, source_target_pairs={{0,16},{16,32},{32,48},{48,64},{64,80},{80,96},{96,112},{112,128},... | collective-permute-start | bytes 18440 | tf_op jit(solution)/shard_map/ppermute | solution.py:15
  39.3 29.9 %copy-start = (bf16[3,384,512]{2,1,0:T(8,128)(2,1)S(1)}, bf16[3,384,512]{2,1,0:T(8,128)(2,1)}, u32[]{:S(2)}) copy-start(bf16[3,384,512]{2,1,0:T(8,128)(2,1)} %param.6) | copy-start | bytes 3538948
  68.7 0.6 copy-start.1
  71.0 5.7 %collective-permute-start.1 = (bf16[127,512]{1,0:T(8,128)(2,1)S(1)}, bf16[127,512]{1,0:T(8,128)(2,1)S(1)}, u32[]{:S(2)}, u32[]{:S(2)}) collective-permute-start(bf16[127,512]{1,0:T(8,128)(2,1)S(1)} %slice_bitcast_fusion.1), channel_id=1, source_target_pairs={{0,16},{16,32},{32,48},{48,64},{64,80},{80,96},{96,112},{112,128},... | collective-permute-start | bytes 390152 | tf_op jit(solution)/shard_map/ppermute | solution.py:15
  76.9 10.4 %copy-start.2 = (f32[512]{0:T(512)S(1)}, f32[512]{0:T(512)}, u32[]{:S(2)}) copy-start(f32[512]{0:T(512)} %param.9) | copy-start | bytes 6148
  86.0 1.8 copy-start.3
  88.8 23.7 %all-to-all-start = ((bf16[32,4,512]{2,1,0:T(4,128)(2,1)}), bf16[32,4,512]{2,1,0:T(4,128)(2,1)S(1)}, u32[]{:S(2)}, u32[]{:S(2)}) async-start(bf16[32,4,512]{2,1,0:T(4,128)(2,1)} %reshape.28), calls=%async_computation | async-start | bytes 262144 | tf_op jit(solution)/shard_map/all_to_all | solution.py:30
  101.5 117.7 %reduce-scatter.2.cloned.1.call-start = ((), (), s32[]{:S(2)}) async-start(), calls=%async_computation.3 | async-start | bytes 7225344 | tf_op jit(solution)/shard_map/reduce_scatter | solution.py:90
  220.3 12.1 %collective-permute-start.2 = (bf16[392,512]{1,0:T(8,128)(2,1)S(1)}, bf16[392,512]{1,0:T(8,128)(2,1)S(1)}, u32[]{:S(2)}, u32[]{:S(2)}) collective-permute-start(bf16[392,512]{1,0:T(8,128)(2,1)S(1)} %constant_dynamic-slice_fusion), channel_id=1, source_target_pairs={{0,1},{1,0},{2,3},{3,2},{4,5},{5,4},{6,7},{7,6},{8,9},{9,8},{10,11... | collective-permute-start | bytes 1204232 | tf_op jit(solution)/shard_map/ppermute | solution.py:23
Sparse Core Ops, SparseCore 0:
  11.1 121.6 all-gather.1
  141.8 77.3 reduce-scatter.1

commit v10 on v8

--- a/solution.py
+++ b/solution.py
@@ -22,6 +22,23 @@
     send = lax.dynamic_slice_in_dim(block, (1 - me) * half, half, 1)
     got = lax.ppermute(send, axis, [(0, 1), (1, 0)])
     return (keep.astype(jnp.float32) + got.astype(jnp.float32)).astype(block.dtype)
+
+
+def halving_scatter(rows, axis):
+    size = lax.axis_size(axis)
+    if size & (size - 1) or rows.shape[0] % size:
+        return exchange_scatter(rows, axis)
+    me = lax.axis_index(axis)
+    step = size // 2
+    while step >= 1:
+        half = rows.shape[0] // 2
+        bit = (me // step) % 2
+        keep = lax.dynamic_slice_in_dim(rows, bit * half, half, 0)
+        send = lax.dynamic_slice_in_dim(rows, (1 - bit) * half, half, 0)
+        pairs = [(i, i ^ step) for i in range(size)]
+        rows = keep + lax.ppermute(send, axis, pairs)
+        step //= 2
+    return rows
 
 
 def exchange_scatter(rows, axis):
@@ -80,7 +97,7 @@
         jnp.bfloat16
     )
     picked_gated = jnp.dot(one_hot, gated, preferred_element_type=jnp.float32)
-    site_gated = exchange_scatter(picked_gated.astype(jnp.bfloat16), "context")
+    site_gated = halving_scatter(picked_gated.astype(jnp.bfloat16), "context")
     gated, site_gated = lax.optimization_barrier((gated, site_gated))
     full_weight = lax.all_gather(out_weight, "context", axis=1, tiled=True)
     sites = site_gated.shape[0]

time: 243 us -> 243 us (level)
  waiting for transfers between devices: 122 us -> 109 us
  starting transfers between devices: 22.6 us -> 35.3 us
    ppermute x0 -> x5, starting transfers between devices: none -> 25.4 us  [halving_scatter(): rows = keep + lax.ppermute(send, axis, pairs)]
    all_gather x1, waiting for transfers between devices: 20.3 us -> 4.76 us  [on_device(): full_weight = lax.all_gather(out_weight, 'context', axis=1, tiled=True)]
    ppermute x0 -> x5, waiting for transfers between devices: none -> 13 us  [halving_scatter(): rows = keep + lax.ppermute(send, axis, pairs)]
    all_to_all x1 -> x0, starting transfers between devices: 12.8 us -> none  [exchange_scatter(): pieces = lax.all_to_all(pieces, axis, 0, 0, tiled=True)]
    all_to_all x1 -> x0, waiting for transfers between devices: 10.8 us -> none  [exchange_scatter(): pieces = lax.all_to_all(pieces, axis, 0, 0, tiled=True)]
  transfers between devices with their start and end apart: 6 -> 10, of which waited for: 5 -> 9; matrix products, arithmetic and copies ran while one was open for 29% -> 29% of each run, Pallas kernels for 0% -> 0%
where the time goes in v10:
time: 243 us; the launch traced here: 242 us
  waiting for transfers between devices  109 us (45%)
  local copies, waits for them, and re-layouts  59.7 us (25%)
  starting transfers between devices  35.3 us (15%)
  matrix products  18.4 us (8%)
  between operations  14.4 us (6%)
  other arithmetic  4.56 us (2%)
    reduce_scatter x1, waiting for transfers between devices, on_device(): partial = lax.psum_scatter(both, 'z', scatter_dimension=1, tiled=True)  78.5 us
    reshape x1, local copies, waits for them, and re-layouts, banded_filters(): return tiled[:, :rows * span].reshape(local_groups, rows, span)  29.3 us
    ppermute x5, starting transfers between devices, halving_scatter(): rows = keep + lax.ppermute(send, axis, pairs)  25.4 us
    unnamed x11, local copies, waits for them, and re-layouts  13.2 us
    ppermute x5, waiting for transfers between devices, halving_scatter(): rows = keep + lax.ppermute(send, axis, pairs)  13 us
    dot_general x1, matrix products, on_device(): jnp.dot(both, full_weight, preferred_element_type=jnp.float32)  9.13 us
    ppermute x1, waiting for transfers between devices, pair_scatter(): got = lax.ppermute(send, axis, [(0, 1), (1, 0)])  9.03 us
    dot_general x1, matrix products, on_device(): jnp.einsum('gim,mgc->igc', toeplitz, extended.reshape(span, local_groups,...  9.02 us
  transfers between devices with their start and end apart: 10, of which 9 were waited for; matrix products, arithmetic and copies ran while one was open for 29% of the time, Pallas kernels for 0%

profile of v10, /device:TPU:1, one launch (start us, length us, event | category | flops | bytes accessed | tf_op | source)
XLA Modules:
  0.0 241.8 jit_solution(8882875923875835668)
XLA Ops:
  8.7 4.6 %collective-permute-start = (bf16[3,2,512]{2,1,0:T(2,128)(2,1)S(1)}, bf16[3,2,512]{2,1,0:T(2,128)(2,1)S(1)}, u32[]{:S(2)}, u32[]{:S(2)}) collective-permute-start(bf16[3,2,512]{2,1,0:T(2,128)(2,1)S(1)} %slice.44), channel_id=1, source_target_pairs={{0,16},{16,32},{32,48},{48,64},{64,80},{80,96},{96,112},{112,128},... | collective-permute-start | bytes 18440 | tf_op jit(solution)/shard_map/ppermute | solution.py:15
  14.2 1.2 broadcast_subtract_fusion
  16.8 5.4 %tile.4 = bf16[32,384,512]{2,1,0:T(8,128)(2,1)} broadcast(bf16[32,512]{1,0:T(8,128)(2,1)S(1)} %concatenate.14), dimensions={0,2} | broadcast | bytes 12615680 | tf_op jit(solution)/shard_map/tile | solution.py:68
  22.2 12.0 %copy.15 = bf16[4,8,384,512]{3,1,2,0:T(8,128)(2,1)S(1)} copy(bf16[4,8,384,512]{3,2,1,0:T(8,128)(2,1)} %bitcast.28) | data formatting | bytes 25165824
  34.2 5.1 %slice.62 = bf16[32,196224]{1,0:T(8,128)(2,1)} slice(bf16[32,196608]{1,0:T(8,128)(2,1)S(1)} %bitcast.29), slice={[0:32], [0:196224]} | slice | bytes 25116672 | tf_op jit(solution)/shard_map/slice | solution.py:69
  39.3 29.3 %reshape.23 = bf16[32,384,511]{2,1,0:T(8,128)(2,1)} reshape(bf16[32,196224]{1,0:T(8,128)(2,1)} %slice.62) | data formatting | bytes 25116672 | tf_op jit(solution)/shard_map/reshape | solution.py:69
  69.3 1.5 multiply_add_fusion
  71.0 2.1 collective-permute-start.1
  73.2 3.4 %collective-permute-done.1 = bf16[127,512]{1,0:T(8,128)(2,1)S(1)} collective-permute-done((bf16[127,512]{1,0:T(8,128)(2,1)S(1)}, bf16[127,512]{1,0:T(8,128)(2,1)S(1)}, u32[]{:S(2)}, u32[]{:S(2)}) %collective-permute-start.1) | collective-permute-done | bytes 130080 | tf_op jit(solution)/shard_map/ppermute | solution.py:15
  77.0 9.0 %fusion.12 = f32[32,16,384]{2,1,0:T(8,128)} fusion(bf16[511,32,16]{0,2,1:T(8,128)(2,1)S(1)} %bitcast.31, bf16[32,384,511]{2,1,0:T(8,128)(2,1)} %reshape.23), kind=kOutput, calls=%fused_computation.39 | convolution fusion | flops 200933376 | bytes 13868032 | tf_op jit(solution)/shard_map/gim,mgc->igc/dot_general | solution.py:86
  86.0 1.4 copy.11
  88.1 3.0 %collective-permute-start.2 = (bf16[64,512]{1,0:T(8,128)(2,1)S(1)}, bf16[64,512]{1,0:T(8,128)(2,1)S(1)}, u32[]{:S(2)}, u32[]{:S(2)}) collective-permute-start(bf16[64,512]{1,0:T(8,128)(2,1)S(1)} %constant_dynamic-slice_fusion.5), channel_id=1, source_target_pairs={{0,256},{16,272},{32,288},{48,304},{64,320},{80,336},{96,352},{112... | collective-permute-start | bytes 196616 | tf_op jit(solution)/shard_map/ppermute | solution.py:39
  91.2 5.2 %collective-permute-done.2 = bf16[64,512]{1,0:T(8,128)(2,1)S(1)} collective-permute-done((bf16[64,512]{1,0:T(8,128)(2,1)S(1)}, bf16[64,512]{1,0:T(8,128)(2,1)S(1)}, u32[]{:S(2)}, u32[]{:S(2)}) %collective-permute-start.2) | collective-permute-done | bytes 65568 | tf_op jit(solution)/shard_map/ppermute | solution.py:39
  96.4 5.3 %collective-permute-start.3 = (bf16[32,512]{1,0:T(8,128)(2,1)S(1)}, bf16[32,512]{1,0:T(8,128)(2,1)S(1)}, u32[]{:S(2)}, u32[]{:S(2)}) collective-permute-start(bf16[32,512]{1,0:T(8,128)(2,1)S(1)} %constant_dynamic-slice_fusion.4), channel_id=1, source_target_pairs={{0,128},{16,144},{32,160},{48,176},{64,192},{80,208},{96,224},{112... | collective-permute-start | bytes 98312 | tf_op jit(solution)/shard_map/ppermute | solution.py:39
  101.8 3.2 %collective-permute-done.3 = bf16[32,512]{1,0:T(8,128)(2,1)S(1)} collective-permute-done((bf16[32,512]{1,0:T(8,128)(2,1)S(1)}, bf16[32,512]{1,0:T(8,128)(2,1)S(1)}, u32[]{:S(2)}, u32[]{:S(2)}) %collective-permute-start.3) | collective-permute-done | bytes 32800 | tf_op jit(solution)/shard_map/ppermute | solution.py:39
  105.0 2.7 %collective-permute-start.4 = (bf16[16,512]{1,0:T(8,128)(2,1)S(1)}, bf16[16,512]{1,0:T(8,128)(2,1)S(1)}, u32[]{:S(2)}, u32[]{:S(2)}) collective-permute-start(bf16[16,512]{1,0:T(8,128)(2,1)S(1)} %constant_dynamic-slice_fusion.3), channel_id=1, source_target_pairs={{0,64},{16,80},{32,96},{48,112},{64,0},{80,16},{96,32},{112,48},{1... | collective-permute-start | bytes 49160 | tf_op jit(solution)/shard_map/ppermute | solution.py:39
  107.8 2.9 %collective-permute-done.4 = bf16[16,512]{1,0:T(8,128)(2,1)S(1)} collective-permute-done((bf16[16,512]{1,0:T(8,128)(2,1)S(1)}, bf16[16,512]{1,0:T(8,128)(2,1)S(1)}, u32[]{:S(2)}, u32[]{:S(2)}) %collective-permute-start.4) | collective-permute-done | bytes 16416 | tf_op jit(solution)/shard_map/ppermute | solution.py:39
  110.7 5.5 %collective-permute-start.5 = (bf16[8,512]{1,0:T(8,128)(2,1)S(1)}, bf16[8,512]{1,0:T(8,128)(2,1)S(1)}, u32[]{:S(2)}, u32[]{:S(2)}) collective-permute-start(bf16[8,512]{1,0:T(8,128)(2,1)S(1)} %constant_dynamic-slice_fusion.2), channel_id=1, source_target_pairs={{0,32},{16,48},{32,0},{48,16},{64,96},{80,112},{96,64},{112,80},{1... | collective-permute-start | bytes 24584 | tf_op jit(solution)/shard_map/ppermute | solution.py:39
  117.3 8.8 %collective-permute-start.6 = (bf16[4,512]{1,0:T(4,128)(2,1)S(1)}, bf16[4,512]{1,0:T(4,128)(2,1)S(1)}, u32[]{:S(2)}, u32[]{:S(2)}) collective-permute-start(bf16[4,512]{1,0:T(4,128)(2,1)S(1)} %constant_dynamic-slice_fusion.1), channel_id=1, source_target_pairs={{0,16},{16,0},{32,48},{48,32},{64,80},{80,64},{96,112},{112,96},{1... | collective-permute-start | bytes 12296 | tf_op jit(solution)/shard_map/ppermute | solution.py:39
  126.9 4.8 %all-gather.2.cloned.1.call-done = bf16[512,8192]{1,0:T(8,128)(2,1)} async-done(((bf16[512,256]{1,0:T(8,128)(2,1)}), bf16[512,8192]{1,0:T(8,128)(2,1)}) %all-gather.2.cloned.1.call-update) | async-done | bytes 8388624 | tf_op jit(solution)/shard_map/all_gather | solution.py:102
  131.7 9.1 %convolution_convert_fusion = bf16[392,8192]{1,0:T(8,128)(2,1)} fusion(bf16[512,8192]{1,0:T(8,128)(2,1)} %all-gather.2.cloned.1.call-done, bf16[4,512]{1,0:T(4,128)(2,1)S(1)} %dynamic-slice_add_fusion.4, bf16[384,512]{1,0:T(8,128)(2,1)S(1)} %fusion.3, bf16[392]{0:T(512)(128)(2,1)S(1)} %pad.3.clone), kind=kOutput, calls=%fused_computation | convolution fusion | flops 3292749824 | bytes 15209232 | tf_op jit(solution)/shard_map/dot_general | solution.py:106
  140.9 78.5 %reduce-scatter.2.cloned.1.call-done = bf16[392,1024]{1,0:T(8,128)(2,1)} async-done(((bf16[392,8192]{1,0:T(8,128)(2,1)}), bf16[392,1024]{1,0:T(8,128)(2,1)}) %reduce-scatter.2.cloned.1.call-update) | async-done | bytes 802832 | tf_op jit(solution)/shard_map/reduce_scatter | solution.py:107
  220.4 3.1 %collective-permute-start.7 = (bf16[392,512]{1,0:T(8,128)(2,1)S(1)}, bf16[392,512]{1,0:T(8,128)(2,1)S(1)}, u32[]{:S(2)}, u32[]{:S(2)}) collective-permute-start(bf16[392,512]{1,0:T(8,128)(2,1)S(1)} %constant_dynamic-slice_fusion), channel_id=1, source_target_pairs={{0,1},{1,0},{2,3},{3,2},{4,5},{5,4},{6,7},{7,6},{8,9},{9,8},{10,11... | collective-permute-start | bytes 1204232 | tf_op jit(solution)/shard_map/ppermute | solution.py:23
  223.5 9.0 %collective-permute-done.7 = bf16[392,512]{1,0:T(8,128)(2,1)S(1)} collective-permute-done((bf16[392,512]{1,0:T(8,128)(2,1)S(1)}, bf16[392,512]{1,0:T(8,128)(2,1)S(1)}, u32[]{:S(2)}, u32[]{:S(2)}) %collective-permute-start.7) | collective-permute-done | bytes 401440 | tf_op jit(solution)/shard_map/ppermute | solution.py:23
  (44 shorter events, 11.0 us)
Async XLA Ops:
  7.2 124.5 %all-gather.2.cloned.1.call-start = ((), (), s32[]{:S(2)}) async-start(), calls=%async_computation.1 | async-start | bytes 8650752 | tf_op jit(solution)/shard_map/all_gather | solution.py:102
  7.9 211.5 %reduce-scatter.2.cloned.1.call-start = ((), (), s32[]{:S(2)}) async-start(), calls=%async_computation.2 | async-start | bytes 7225344 | tf_op jit(solution)/shard_map/reduce_scatter | solution.py:107
  8.7 60.0 %collective-permute-start = (bf16[3,2,512]{2,1,0:T(2,128)(2,1)S(1)}, bf16[3,2,512]{2,1,0:T(2,128)(2,1)S(1)}, u32[]{:S(2)}, u32[]{:S(2)}) collective-permute-start(bf16[3,2,512]{2,1,0:T(2,128)(2,1)S(1)} %slice.44), channel_id=1, source_target_pairs={{0,16},{16,32},{32,48},{48,64},{64,80},{80,96},{96,112},{112,128},... | collective-permute-start | bytes 18440 | tf_op jit(solution)/shard_map/ppermute | solution.py:15
  39.3 29.9 %copy-start = (bf16[3,384,512]{2,1,0:T(8,128)(2,1)S(1)}, bf16[3,384,512]{2,1,0:T(8,128)(2,1)}, u32[]{:S(2)}) copy-start(bf16[3,384,512]{2,1,0:T(8,128)(2,1)} %param.6) | copy-start | bytes 3538948
  68.7 0.6 copy-start.1
  71.0 5.7 %collective-permute-start.1 = (bf16[127,512]{1,0:T(8,128)(2,1)S(1)}, bf16[127,512]{1,0:T(8,128)(2,1)S(1)}, u32[]{:S(2)}, u32[]{:S(2)}) collective-permute-start(bf16[127,512]{1,0:T(8,128)(2,1)S(1)} %slice_bitcast_fusion.1), channel_id=1, source_target_pairs={{0,16},{16,32},{32,48},{48,64},{64,80},{80,96},{96,112},{112,128},... | collective-permute-start | bytes 390152 | tf_op jit(solution)/shard_map/ppermute | solution.py:15
  77.0 10.5 %copy-start.2 = (f32[512]{0:T(512)S(1)}, f32[512]{0:T(512)}, u32[]{:S(2)}) copy-start(f32[512]{0:T(512)} %param.9) | copy-start | bytes 6148
  86.0 1.8 copy-start.3
  88.1 8.3 %collective-permute-start.2 = (bf16[64,512]{1,0:T(8,128)(2,1)S(1)}, bf16[64,512]{1,0:T(8,128)(2,1)S(1)}, u32[]{:S(2)}, u32[]{:S(2)}) collective-permute-start(bf16[64,512]{1,0:T(8,128)(2,1)S(1)} %constant_dynamic-slice_fusion.5), channel_id=1, source_target_pairs={{0,256},{16,272},{32,288},{48,304},{64,320},{80,336},{96,352},{112... | collective-permute-start | bytes 196616 | tf_op jit(solution)/shard_map/ppermute | solution.py:39
  96.4 8.6 %collective-permute-start.3 = (bf16[32,512]{1,0:T(8,128)(2,1)S(1)}, bf16[32,512]{1,0:T(8,128)(2,1)S(1)}, u32[]{:S(2)}, u32[]{:S(2)}) collective-permute-start(bf16[32,512]{1,0:T(8,128)(2,1)S(1)} %constant_dynamic-slice_fusion.4), channel_id=1, source_target_pairs={{0,128},{16,144},{32,160},{48,176},{64,192},{80,208},{96,224},{112... | collective-permute-start | bytes 98312 | tf_op jit(solution)/shard_map/ppermute | solution.py:39
  105.0 5.7 %collective-permute-start.4 = (bf16[16,512]{1,0:T(8,128)(2,1)S(1)}, bf16[16,512]{1,0:T(8,128)(2,1)S(1)}, u32[]{:S(2)}, u32[]{:S(2)}) collective-permute-start(bf16[16,512]{1,0:T(8,128)(2,1)S(1)} %constant_dynamic-slice_fusion.3), channel_id=1, source_target_pairs={{0,64},{16,80},{32,96},{48,112},{64,0},{80,16},{96,32},{112,48},{1... | collective-permute-start | bytes 49160 | tf_op jit(solution)/shard_map/ppermute | solution.py:39
  110.7 6.6 %collective-permute-start.5 = (bf16[8,512]{1,0:T(8,128)(2,1)S(1)}, bf16[8,512]{1,0:T(8,128)(2,1)S(1)}, u32[]{:S(2)}, u32[]{:S(2)}) collective-permute-start(bf16[8,512]{1,0:T(8,128)(2,1)S(1)} %constant_dynamic-slice_fusion.2), channel_id=1, source_target_pairs={{0,32},{16,48},{32,0},{48,16},{64,96},{80,112},{96,64},{112,80},{1... | collective-permute-start | bytes 24584 | tf_op jit(solution)/shard_map/ppermute | solution.py:39
  117.3 9.6 %collective-permute-start.6 = (bf16[4,512]{1,0:T(4,128)(2,1)S(1)}, bf16[4,512]{1,0:T(4,128)(2,1)S(1)}, u32[]{:S(2)}, u32[]{:S(2)}) collective-permute-start(bf16[4,512]{1,0:T(4,128)(2,1)S(1)} %constant_dynamic-slice_fusion.1), channel_id=1, source_target_pairs={{0,16},{16,0},{32,48},{48,32},{64,80},{80,64},{96,112},{112,96},{1... | collective-permute-start | bytes 12296 | tf_op jit(solution)/shard_map/ppermute | solution.py:39
  220.4 12.1 %collective-permute-start.7 = (bf16[392,512]{1,0:T(8,128)(2,1)S(1)}, bf16[392,512]{1,0:T(8,128)(2,1)S(1)}, u32[]{:S(2)}, u32[]{:S(2)}) collective-permute-start(bf16[392,512]{1,0:T(8,128)(2,1)S(1)} %constant_dynamic-slice_fusion), channel_id=1, source_target_pairs={{0,1},{1,0},{2,3},{3,2},{4,5},{5,4},{6,7},{7,6},{8,9},{9,8},{10,11... | collective-permute-start | bytes 1204232 | tf_op jit(solution)/shard_map/ppermute | solution.py:23
Sparse Core Ops, SparseCore 0:
  11.1 120.5 all-gather.1
  141.0 78.3 reduce-scatter.1
